TPU v7x, 512 devices: a whole 4x8x8 slice. The times are simulated.
512 devices in a mesh: resp: 64 (over y_lo, z, core), mp: 8 (over y_hi, x).
Axes of the slice: x: 4, y: 8 (y_hi: 2, y_lo: 4; y = y_hi * 4 + y_lo), z: 8, core: 2. Of those that a mesh axis runs over, the one named last changes fastest.
Arguments:
- queries: bfloat16 [16384, 64, 128], P('resp', 'mp'), may hold values from -200 to 200
- response_kv: bfloat16 [16384, 2, 8, 128], P('resp', None, 'mp'), may hold values from -6 to 6
- prefix_kv: bfloat16 [4096, 2, 8, 128], P(('resp', 'mp')), may hold values from -8 to 8
- lengths: int32 [64], P('resp'), may hold values from 128 to 256, as said below
- score_weight: float32 [8192], P('mp'), may hold values from -30 to 30
Outputs:
- attended: bfloat16 [16384, 8192], P('resp', 'mp')
- score: float32 [64], P('resp')
Inputs may be any that keep to these rules, and one draw needn't show every extreme that they name: `lengths`: every length is a multiple of 128; some response is full and some has one tile.
All inputs are finite; a program needn't handle non-finite values.
Results may differ from a plain program's by a relative error of at most 0.0045.
Values may be sent and summed in bfloat16 or wider, within the bound.
No kernel may reach another device: no remote copies, remote signals or barrier semaphores. Data moves between devices by JAX's collectives and lax.ppermute only.
A program may use at most 64 MiB of HBM per device.

v0:
```python
import math

import jax
import jax.numpy as jnp
from jax import lax
from jax.sharding import PartitionSpec as P

neg_large = -1e30


def absorb(carry, keys, values, grouped, factor):
    best, total, accum = carry
    scores = jnp.einsum("grd,sgd->grs", grouped, keys, preferred_element_type=jnp.float32) * factor
    fresh = jnp.maximum(best, jnp.max(scores, axis=-1, keepdims=True))
    shrink = jnp.exp(best - fresh)
    weights = jnp.exp(scores - fresh)
    total = total * shrink + jnp.sum(weights, axis=-1, keepdims=True)
    accum = accum * shrink + jnp.einsum(
        "grs,sgd->grd", weights.astype(jnp.bfloat16), values, preferred_element_type=jnp.float32
    )
    return (fresh, total, accum)


def sweep(carry, whole_cache, grouped, factor):
    count = whole_cache.shape[0]
    block_len = math.gcd(count, 512)
    blocks = whole_cache.reshape((count // block_len, block_len) + whole_cache.shape[1:])

    def one_block(state, block):
        return (absorb(state, block[:, 0], block[:, 1], grouped, factor), None)

    carry, unused = lax.scan(one_block, carry, blocks)
    return carry


def per_device(queries, response_kv, prefix_kv, lengths, score_weight):
    resp_len = queries.shape[0]
    local_heads = queries.shape[1]
    head_size = queries.shape[2]
    local_kv = response_kv.shape[2]
    group = local_heads // local_kv
    rows = group * resp_len
    factor = 1.0 / math.sqrt(head_size)
    length = lengths[0]
    grouped = jnp.transpose(
        queries.reshape(resp_len, local_kv, group, head_size), (1, 2, 0, 3)
    ).reshape(local_kv, rows, head_size)
    key_pos = jnp.arange(resp_len, dtype=jnp.int32)[None, :]
    query_pos = (jnp.arange(rows, dtype=jnp.int32) % resp_len)[:, None]
    allowed = ((key_pos <= query_pos) & (key_pos < length))[None]
    near = (
        jnp.einsum("grd,sgd->grs", grouped, response_kv[:, 0], preferred_element_type=jnp.float32)
        * factor
    )
    near = jnp.where(allowed, near, neg_large)
    best = jnp.max(near, axis=-1, keepdims=True)
    near_w = jnp.where(allowed, jnp.exp(near - best), 0.0)
    total = jnp.sum(near_w, axis=-1, keepdims=True)
    accum = jnp.einsum(
        "grs,sgd->grd",
        near_w.astype(jnp.bfloat16),
        response_kv[:, 1],
        preferred_element_type=jnp.float32,
    )
    start_state = (best, total, accum)
    mine = lax.all_to_all(prefix_kv, "mp", split_axis=2, concat_axis=0, tiled=True)
    collected = lax.all_gather(mine, "resp", axis=0, tiled=True)
    best, total, accum = sweep(start_state, collected, grouped, factor)
    mixed = (accum / total).reshape(local_kv, group, resp_len, head_size)
    mixed = jnp.transpose(mixed, (2, 0, 1, 3)).reshape(resp_len, local_heads * head_size)
    live = jnp.arange(resp_len, dtype=jnp.int32)[:, None] < length
    attended = jnp.where(live, mixed, 0.0).astype(jnp.bfloat16)
    partial_score = jnp.sum(attended.astype(jnp.float32) * score_weight[None, :])
    summed = lax.psum(partial_score, "mp")
    score = (summed / length.astype(jnp.float32)).reshape(1)
    return (attended, score)


def solution(mesh):
    in_specs = (
        P("resp", "mp", None),
        P("resp", None, "mp", None),
        P(("resp", "mp"), None, None, None),
        P("resp"),
        P("mp"),
    )
    out_specs = (P("resp", "mp"), P("resp"))
    return jax.shard_map(
        per_device, mesh=mesh, in_specs=in_specs, out_specs=out_specs, check_vma=False
    )
```

profile of v0, /device:TPU:8, one launch (start us, length us, event | category | flops | bytes accessed | tf_op | source)
XLA Modules:
  0.0 215.8 jit_solution(12020379419026221911)
XLA Ops:
  7.2 0.8 copy.18
  8.0 18.6 %all_to_all.18 = bf16[8,2,8,128]{3,0,1,2:T(8,128)(2,1)S(1)} all-to-all(bf16[8,2,8,128]{3,0,1,2:T(8,128)(2,1)S(1)} %copy.18), channel_id=1, replica_groups=mesh['resp'=64,'mp'=8] {'mp'}, dimensions={2} | all-to-all | bytes 65536 | tf_op jit(solution)/shard_map/all_to_all | solution.py:66
  27.9 1.1 copy.15
  29.0 1.2 fusion.24
  31.7 1.0 convolution_bitcast_fusion.1
  32.6 110.5 %all-gather.2.cloned.1.call-done = bf16[4096,2,1,128]{3,0,1,2:T(8,128)(2,1)} async-done(((bf16[64,2,1,128]{3,0,1,2:T(8,128)(2,1)}), bf16[4096,2,1,128]{3,0,1,2:T(8,128)(2,1)}) %all-gather.2.cloned.1.call-update) | async-done | bytes 2097168 | tf_op jit(solution)/shard_map/all_gather | solution.py:67
  143.2 29.5 %while.14 = (s32[]{:T(128)}, f32[1,2048,1]{1,2,0:T(1,128)S(1)}, f32[1,2048,1]{1,2,0:T(1,128)S(1)}, f32[1,2048,128]{2,1,0:T(8,128)S(1)}, bf16[8,512,2,1,128]{4,1,...) while((s32[]{:T(128)}, f32[1,2048,1]{1,2,0:T(1,128)S(1)}, f32[1,2048,1]{1,2,0:T(1,128)S(1)}, ...), condition=%wide.region_5.6_spmd, body=%wide.region_2.5_spmd.sunk | while | flops 545787904 | bytes 16121945 | solution.py:32
  143.2 1.0 dynamic-slice_bitcast_fusion.2
  144.2 0.7 multiply_reduce_fusion.3
  145.7 1.2 fusion.32
  146.9 1.0 dynamic-slice_bitcast_fusion.2
  147.8 0.7 multiply_reduce_fusion.3
  149.3 1.2 fusion.32
  150.6 1.0 dynamic-slice_bitcast_fusion.2
  153.0 1.2 fusion.32
  154.2 1.0 dynamic-slice_bitcast_fusion.2
  155.2 0.7 multiply_reduce_fusion.3
  156.7 1.2 fusion.32
  157.9 1.0 dynamic-slice_bitcast_fusion.2
  158.9 0.7 multiply_reduce_fusion.3
  160.4 1.2 fusion.32
  161.6 1.0 dynamic-slice_bitcast_fusion.2
  164.1 1.2 fusion.32
  165.3 1.0 dynamic-slice_bitcast_fusion.2
  166.3 0.7 multiply_reduce_fusion.3
  167.8 1.2 fusion.32
  169.0 1.0 dynamic-slice_bitcast_fusion.2
  170.0 0.7 multiply_reduce_fusion.3
  171.5 1.2 fusion.32
  173.0 1.0 multiply_reduce_fusion.1
  174.4 31.9 %psum.7 = f32[]{:T(128)} all-reduce(f32[]{:T(128)} %multiply_reduce_fusion.1), channel_id=1, replica_groups=mesh['resp'=64,'mp'=8] {'mp'}, use_global_device_ids=true, to_apply=%region_7.8 | all-reduce | flops 1 | bytes 8 | tf_op jit(solution)/shard_map/psum | solution.py:74
  206.2 1.0 fusion.14
  (45 shorter events, 10.3 us)
Async XLA Ops:
  7.2 136.0 %all-gather.2.cloned.1.call-start = ((), (), s32[]{:S(2)}) async-start(), calls=%async_computation.1 | async-start | bytes 2129920 | tf_op jit(solution)/shard_map/all_gather | solution.py:67
  143.2 29.8 %copy-start = (f32[1024]{0:T(1024)S(1)}, f32[1024]{0:T(1024)}, u32[]{:S(2)}) copy-start(f32[1024]{0:T(1024)} %param.11) | copy-start | bytes 12292
Sparse Core Ops, SparseCore 0:
  27.4 115.7 all-gather.1
where the time goes:
time: 216 us
  waiting for transfers between devices  111 us (51%)
  blocking collectives  50.5 us (23%)
  matrix products  16.9 us (8%)
  between operations  16.5 us (8%)
  local copies, waits for them, and re-layouts  11.9 us (6%)
  other arithmetic  9.04 us (4%)
    all_gather x1, waiting for transfers between devices, per_device(): collected = lax.all_gather(mine, 'resp', axis=0, tiled=True)  111 us
    psum x1, blocking collectives, per_device(): summed = lax.psum(partial_score, 'mp')  31.9 us
    all_to_all x1, blocking collectives, per_device(): lax.all_to_all(prefix_kv, 'mp', split_axis=2, concat_axis=0, tiled=True)  18.6 us
    dot_general x8, matrix products, absorb(): jnp.einsum('grs,sgd->grd', weights.astype(jnp.bfloat16), values, preferre...  9.46 us
    squeeze x8, local copies, waits for them, and re-layouts, sweep(): carry, unused = lax.scan(one_block, carry, blocks)  7.82 us
    dot_general x8, matrix products, absorb(): jnp.einsum('grd,sgd->grs', grouped, keys, preferred_element_type=jnp.floa...  5.75 us
    reduce_sum x8, other arithmetic, absorb(): total = total * shrink + jnp.sum(weights, axis=-1, keepdims=True)  5.68 us
  transfers between devices with their start and end apart: 1, of which 1 were waited for; matrix products, arithmetic and copies ran while one was open for 2% of the time, Pallas kernels for 0%

commit v1 on v0

--- a/solution.py
+++ b/solution.py
@@ -2,10 +2,24 @@
 
 import jax
 import jax.numpy as jnp
+import numpy as np
 from jax import lax
 from jax.sharding import PartitionSpec as P
 
 neg_large = -1e30
+
+resp_parts = (("y_lo", 4), ("z", 8), ("core", 2))
+mp_parts = (("y_hi", 2), ("x", 4))
+resp_axes = tuple(name for name, _ in resp_parts)
+mp_axes = tuple(name for name, _ in mp_parts)
+axis_size = dict(resp_parts + mp_parts)
+
+
+def gather_by_all_to_all(x, axes):
+    count = int(np.prod([axis_size[a] for a in axes]))
+    copies = jnp.broadcast_to(x[None], (count,) + x.shape)
+    got = lax.all_to_all(copies, axes, 0, 0, tiled=True)
+    return got.reshape((count * x.shape[0],) + x.shape[1:])
 
 
 def absorb(carry, keys, values, grouped, factor):
@@ -63,28 +77,32 @@
         preferred_element_type=jnp.float32,
     )
     start_state = (best, total, accum)
-    mine = lax.all_to_all(prefix_kv, "mp", split_axis=2, concat_axis=0, tiled=True)
-    collected = lax.all_gather(mine, "resp", axis=0, tiled=True)
+    mine = lax.all_to_all(prefix_kv, mp_axes, split_axis=2, concat_axis=0, tiled=True)
+    collected = gather_by_all_to_all(gather_by_all_to_all(mine, ("y_lo", "z")), ("core",))
     best, total, accum = sweep(start_state, collected, grouped, factor)
     mixed = (accum / total).reshape(local_kv, group, resp_len, head_size)
     mixed = jnp.transpose(mixed, (2, 0, 1, 3)).reshape(resp_len, local_heads * head_size)
     live = jnp.arange(resp_len, dtype=jnp.int32)[:, None] < length
     attended = jnp.where(live, mixed, 0.0).astype(jnp.bfloat16)
     partial_score = jnp.sum(attended.astype(jnp.float32) * score_weight[None, :])
-    summed = lax.psum(partial_score, "mp")
+    spread = jnp.broadcast_to(partial_score, (axis_size["y_hi"] * axis_size["x"],))
+    summed = jnp.sum(lax.all_to_all(spread, mp_axes, 0, 0, tiled=True))
     score = (summed / length.astype(jnp.float32)).reshape(1)
     return (attended, score)
 
 
 def solution(mesh):
+    sizes = tuple(n for _, n in resp_parts) + tuple(n for _, n in mp_parts)
+    fine = jax.sharding.Mesh(np.asarray(mesh.devices).reshape(sizes), resp_axes + mp_axes)
+    R, M = resp_axes, mp_axes
     in_specs = (
-        P("resp", "mp", None),
-        P("resp", None, "mp", None),
-        P(("resp", "mp"), None, None, None),
-        P("resp"),
-        P("mp"),
+        P(R, M, None),
+        P(R, None, M, None),
+        P(R + M, None, None, None),
+        P(R),
+        P(M),
     )
-    out_specs = (P("resp", "mp"), P("resp"))
+    out_specs = (P(R, M), P(R))
     return jax.shard_map(
-        per_device, mesh=mesh, in_specs=in_specs, out_specs=out_specs, check_vma=False
+        per_device, mesh=fine, in_specs=in_specs, out_specs=out_specs, check_vma=False
     )

time: 216 us -> 116 us (0.54)
  the two profiles are of different devices: /device:TPU:8 before, /device:TPU:16 now
where the time goes in v1:
time: 116 us; the launch traced here: 115 us
  waiting for transfers between devices  31.6 us (27%)
  blocking collectives  23.1 us (20%)
  matrix products  16.9 us (15%)
  starting transfers between devices  16.3 us (14%)
  local copies, waits for them, and re-layouts  13.6 us (12%)
  other arithmetic  9.65 us (8%)
  between operations  3.21 us (3%)
    all_to_all x1, waiting for transfers between devices, gather_by_all_to_all(): got = lax.all_to_all(copies, axes, 0, 0, tiled=True)  22.6 us
    all_to_all x1, blocking collectives, per_device(): lax.all_to_all(prefix_kv, mp_axes, split_axis=2, concat_axis=0, tiled=True)  17.7 us
    all_to_all x1, starting transfers between devices, gather_by_all_to_all(): got = lax.all_to_all(copies, axes, 0, 0, tiled=True)  12.9 us
    dot_general x8, matrix products, absorb(): jnp.einsum('grs,sgd->grd', weights.astype(jnp.bfloat16), values, preferre...  9.46 us
    all_to_all x1, waiting for transfers between devices, per_device(): summed = jnp.sum(lax.all_to_all(spread, mp_axes, 0, 0, tiled=True))  9.07 us
    squeeze x8, local copies, waits for them, and re-layouts, sweep(): carry, unused = lax.scan(one_block, carry, blocks)  7.8 us
    dot_general x8, matrix products, absorb(): jnp.einsum('grd,sgd->grs', grouped, keys, preferred_element_type=jnp.floa...  5.75 us
    reduce_sum x8, other arithmetic, absorb(): total = total * shrink + jnp.sum(weights, axis=-1, keepdims=True)  5.68 us
  transfers between devices with their start and end apart: 2, of which 2 were waited for; matrix products, arithmetic and copies ran while one was open for 3% of the time, Pallas kernels for 0%

profile of v1, /device:TPU:16, one launch (start us, length us, event | category | flops | bytes accessed | tf_op | source)
XLA Modules:
  0.0 114.8 jit_solution(14273344638396157346)
XLA Ops:
  0.6 0.8 copy.44
  1.5 17.7 %all_to_all.31 = bf16[8,2,8,128]{3,0,1,2:T(8,128)(2,1)S(1)} all-to-all(bf16[8,2,8,128]{3,0,1,2:T(8,128)(2,1)S(1)} %copy.44), channel_id=1, replica_groups=mesh['y_lo'=4,'z'=8,'core'=2,'y_hi'=2,'x'=4] {'y_hi','x'}, dimensions={2} | all-to-all | bytes 65536 | tf_op jit(solution)/shard_map/all_to_all | solution.py:80
  19.2 1.2 %broadcast_in_dim.64 = bf16[32,64,2,1,128]{4,1,2,3,0:T(8,128)(2,1)} broadcast(bf16[64,2,128]{2,0,1:T(8,128)(2,1)S(1)} %bitcast.107), dimensions={1,2,4} | broadcast | bytes 1081344 | tf_op jit(solution)/shard_map/broadcast_in_dim | solution.py:20
  20.4 12.9 %all-to-all-start.1 = ((bf16[32,64,2,1,128]{4,1,2,3,0:T(8,128)(2,1)}), bf16[32,64,2,1,128]{4,1,2,3,0:T(8,128)(2,1)S(1)}, u32[]{:S(2)}, u32[]{:S(2)}) async-start(bf16[32,64,2,1,128]{4,1,2,3,0:T(8,128)(2,1)} %broadcast_in_dim.64), calls=%async_computation.1 | async-start | bytes 2097152 | tf_op jit(solution)/shard_map/all_to_all | solution.py:21
  35.8 1.0 convolution_bitcast_fusion.1
  36.8 22.6 %all-to-all-done.1 = bf16[32,64,2,1,128]{4,1,2,3,0:T(8,128)(2,1)S(1)} async-done(((bf16[32,64,2,1,128]{4,1,2,3,0:T(8,128)(2,1)}), bf16[32,64,2,1,128]{4,1,2,3,0:T(8,128)(2,1)S(1)}, u32[]{:S(2)}, u32[]{:S(2)}) %all-to-all-start.1) | async-done | bytes 1048608 | tf_op jit(solution)/shard_map/all_to_all | solution.py:21
  59.7 5.4 %all_to_all.32 = bf16[2,2048,2,1,128]{4,1,2,3,0:T(8,128)(2,1)S(1)} all-to-all(bf16[2,2048,2,1,128]{4,1,2,3,0:T(8,128)(2,1)S(1)} %broadcast_in_dim.66), channel_id=1, replica_groups=mesh['y_lo'=4,'z'=8,'core'=2,'y_hi'=2,'x'=4] {'core'}, dimensions={0} | all-to-all | bytes 4194304 | tf_op jit(solution)/shard_map/all_to_all | solution.py:21
  65.1 1.5 %copy.47 = bf16[2,2048,2,1,128]{4,1,0,2,3:T(8,128)(2,1)} copy(bf16[2,2048,2,1,128]{4,1,2,3,0:T(8,128)(2,1)S(1)} %all_to_all.32) | data formatting | bytes 4194304 | tf_op jit(solution)/shard_map/all_to_all | solution.py:21
  66.6 29.5 %while.14 = (s32[]{:T(128)}, f32[1,2048,1]{1,2,0:T(1,128)S(1)}, f32[1,2048,1]{1,2,0:T(1,128)S(1)}, f32[1,2048,128]{2,1,0:T(8,128)S(1)}, bf16[8,512,2,1,128]{4,1,...) while((s32[]{:T(128)}, f32[1,2048,1]{1,2,0:T(1,128)S(1)}, f32[1,2048,1]{1,2,0:T(1,128)S(1)}, ...), condition=%wide.region_5.6_spmd, body=%wide.region_2.5_spmd.sunk | while | flops 545787904 | bytes 16121945 | solution.py:46
  66.6 1.0 dynamic-slice_bitcast_fusion.2
  69.1 1.2 %fusion.32 = f32[1,2048,128]{2,1,0:T(8,128)S(1)} fusion(f32[512,2048]{1,0:T(8,128)S(1)} %get-tuple-element.129, f32[2048]{0:T(1024)S(1)} %bitcast.96, f32[1,2048,128]{2,1,0:T(8,128)S(1)} %get-tuple-element.142, f32[2048]{0:T(1024)S(1)} %bitcast.103, bf16[512,2,1,128]{3,0,2,1:T(8,128)(2,1)S(1)} %dynamic-slice_bitcast_fusion.2), kind=kOutput, calls=%fused_computation.5.clone.1 | convolution fusion | flops 272105472 | bytes 6438912 | tf_op jit(solution)/shard_map/while/body/eval_jaxpr/grs,sgd->grd/dot_general | solution.py:32
  70.3 1.0 dynamic-slice_bitcast_fusion.2
  72.7 1.2 %fusion.32 = f32[1,2048,128]{2,1,0:T(8,128)S(1)} fusion(f32[512,2048]{1,0:T(8,128)S(1)} %get-tuple-element.129, f32[2048]{0:T(1024)S(1)} %bitcast.96, f32[1,2048,128]{2,1,0:T(8,128)S(1)} %get-tuple-element.142, f32[2048]{0:T(1024)S(1)} %bitcast.103, bf16[512,2,1,128]{3,0,2,1:T(8,128)(2,1)S(1)} %dynamic-slice_bitcast_fusion.2), kind=kOutput, calls=%fused_computation.5.clone.1 | convolution fusion | flops 272105472 | bytes 6438912 | tf_op jit(solution)/shard_map/while/body/eval_jaxpr/grs,sgd->grd/dot_general | solution.py:32
  74.0 1.0 dynamic-slice_bitcast_fusion.2
  74.9 0.7 multiply_reduce_fusion.3
  76.4 1.2 %fusion.32 = f32[1,2048,128]{2,1,0:T(8,128)S(1)} fusion(f32[512,2048]{1,0:T(8,128)S(1)} %get-tuple-element.129, f32[2048]{0:T(1024)S(1)} %bitcast.96, f32[1,2048,128]{2,1,0:T(8,128)S(1)} %get-tuple-element.142, f32[2048]{0:T(1024)S(1)} %bitcast.103, bf16[512,2,1,128]{3,0,2,1:T(8,128)(2,1)S(1)} %dynamic-slice_bitcast_fusion.2), kind=kOutput, calls=%fused_computation.5.clone.1 | convolution fusion | flops 272105472 | bytes 6438912 | tf_op jit(solution)/shard_map/while/body/eval_jaxpr/grs,sgd->grd/dot_general | solution.py:32
  77.6 1.0 dynamic-slice_bitcast_fusion.2
  80.1 1.2 %fusion.32 = f32[1,2048,128]{2,1,0:T(8,128)S(1)} fusion(f32[512,2048]{1,0:T(8,128)S(1)} %get-tuple-element.129, f32[2048]{0:T(1024)S(1)} %bitcast.96, f32[1,2048,128]{2,1,0:T(8,128)S(1)} %get-tuple-element.142, f32[2048]{0:T(1024)S(1)} %bitcast.103, bf16[512,2,1,128]{3,0,2,1:T(8,128)(2,1)S(1)} %dynamic-slice_bitcast_fusion.2), kind=kOutput, calls=%fused_computation.5.clone.1 | convolution fusion | flops 272105472 | bytes 6438912 | tf_op jit(solution)/shard_map/while/body/eval_jaxpr/grs,sgd->grd/dot_general | solution.py:32
  81.3 1.0 dynamic-slice_bitcast_fusion.2
  83.8 1.2 %fusion.32 = f32[1,2048,128]{2,1,0:T(8,128)S(1)} fusion(f32[512,2048]{1,0:T(8,128)S(1)} %get-tuple-element.129, f32[2048]{0:T(1024)S(1)} %bitcast.96, f32[1,2048,128]{2,1,0:T(8,128)S(1)} %get-tuple-element.142, f32[2048]{0:T(1024)S(1)} %bitcast.103, bf16[512,2,1,128]{3,0,2,1:T(8,128)(2,1)S(1)} %dynamic-slice_bitcast_fusion.2), kind=kOutput, calls=%fused_computation.5.clone.1 | convolution fusion | flops 272105472 | bytes 6438912 | tf_op jit(solution)/shard_map/while/body/eval_jaxpr/grs,sgd->grd/dot_general | solution.py:32
  85.0 1.0 dynamic-slice_bitcast_fusion.2
  86.0 0.7 multiply_reduce_fusion.3
  87.5 1.2 %fusion.32 = f32[1,2048,128]{2,1,0:T(8,128)S(1)} fusion(f32[512,2048]{1,0:T(8,128)S(1)} %get-tuple-element.129, f32[2048]{0:T(1024)S(1)} %bitcast.96, f32[1,2048,128]{2,1,0:T(8,128)S(1)} %get-tuple-element.142, f32[2048]{0:T(1024)S(1)} %bitcast.103, bf16[512,2,1,128]{3,0,2,1:T(8,128)(2,1)S(1)} %dynamic-slice_bitcast_fusion.2), kind=kOutput, calls=%fused_computation.5.clone.1 | convolution fusion | flops 272105472 | bytes 6438912 | tf_op jit(solution)/shard_map/while/body/eval_jaxpr/grs,sgd->grd/dot_general | solution.py:32
  88.7 1.0 dynamic-slice_bitcast_fusion.2
  91.2 1.2 %fusion.32 = f32[1,2048,128]{2,1,0:T(8,128)S(1)} fusion(f32[512,2048]{1,0:T(8,128)S(1)} %get-tuple-element.129, f32[2048]{0:T(1024)S(1)} %bitcast.96, f32[1,2048,128]{2,1,0:T(8,128)S(1)} %get-tuple-element.142, f32[2048]{0:T(1024)S(1)} %bitcast.103, bf16[512,2,1,128]{3,0,2,1:T(8,128)(2,1)S(1)} %dynamic-slice_bitcast_fusion.2), kind=kOutput, calls=%fused_computation.5.clone.1 | convolution fusion | flops 272105472 | bytes 6438912 | tf_op jit(solution)/shard_map/while/body/eval_jaxpr/grs,sgd->grd/dot_general | solution.py:32
  92.4 1.0 dynamic-slice_bitcast_fusion.2
  94.9 1.2 %fusion.32 = f32[1,2048,128]{2,1,0:T(8,128)S(1)} fusion(f32[512,2048]{1,0:T(8,128)S(1)} %get-tuple-element.129, f32[2048]{0:T(1024)S(1)} %bitcast.96, f32[1,2048,128]{2,1,0:T(8,128)S(1)} %get-tuple-element.142, f32[2048]{0:T(1024)S(1)} %bitcast.103, bf16[512,2,1,128]{3,0,2,1:T(8,128)(2,1)S(1)} %dynamic-slice_bitcast_fusion.2), kind=kOutput, calls=%fused_computation.5.clone.1 | convolution fusion | flops 272105472 | bytes 6438912 | tf_op jit(solution)/shard_map/while/body/eval_jaxpr/grs,sgd->grd/dot_general | solution.py:32
  96.8 1.0 multiply_reduce_fusion.1
  97.8 1.2 %broadcast_in_dim.70 = f32[8,1,1]{2,1,0:T(1,128)} broadcast(f32[]{:T(128)} %multiply_reduce_fusion.1), dimensions={} | broadcast | bytes 36 | tf_op jit(solution)/shard_map/broadcast_in_dim | solution.py:88
  99.0 3.3 %all-to-all-start.3 = ((f32[8,1,1]{2,1,0:T(1,128)}), f32[8,1,1]{2,1,0:T(1,128)S(1)}, u32[]{:S(2)}, u32[]{:S(2)}) async-start(f32[8,1,1]{2,1,0:T(1,128)} %broadcast_in_dim.70), calls=%async_computation.3 | async-start | bytes 8192 | tf_op jit(solution)/shard_map/all_to_all | solution.py:89
  102.4 1.0 fusion.14
  103.3 9.1 %all-to-all-done.3 = f32[8,1,1]{2,1,0:T(1,128)S(1)} async-done(((f32[8,1,1]{2,1,0:T(1,128)}), f32[8,1,1]{2,1,0:T(1,128)S(1)}, u32[]{:S(2)}, u32[]{:S(2)}) %all-to-all-start.3) | async-done | bytes 64 | tf_op jit(solution)/shard_map/all_to_all | solution.py:89
  (56 shorter events, 13.7 us)
Async XLA Ops:
  0.6 33.4 %copy-start = (bf16[256,8,128]{2,1,0:T(8,128)(2,1)S(1)}, bf16[256,8,128]{2,1,0:T(8,128)(2,1)}, u32[]{:S(2)}) copy-start(bf16[256,8,128]{2,1,0:T(8,128)(2,1)} %param.7) | copy-start | bytes 1572868
  19.2 15.0 %copy-start.1 = (bf16[256,2,1,128]{3,1,2,0:T(2,128)(2,1)S(1)}, bf16[256,2,1,128]{3,1,2,0:T(2,128)(2,1)}, u32[]{:S(2)}) copy-start(bf16[256,2,1,128]{3,1,2,0:T(2,128)(2,1)} %param.8) | copy-start | bytes 393220
  20.4 38.9 %all-to-all-start.1 = ((bf16[32,64,2,1,128]{4,1,2,3,0:T(8,128)(2,1)}), bf16[32,64,2,1,128]{4,1,2,3,0:T(8,128)(2,1)S(1)}, u32[]{:S(2)}, u32[]{:S(2)}) async-start(bf16[32,64,2,1,128]{4,1,2,3,0:T(8,128)(2,1)} %broadcast_in_dim.64), calls=%async_computation.1 | async-start | bytes 2097152 | tf_op jit(solution)/shard_map/all_to_all | solution.py:21
  96.1 0.7 copy-start.2
  99.0 13.4 %all-to-all-start.3 = ((f32[8,1,1]{2,1,0:T(1,128)}), f32[8,1,1]{2,1,0:T(1,128)S(1)}, u32[]{:S(2)}, u32[]{:S(2)}) async-start(f32[8,1,1]{2,1,0:T(1,128)} %broadcast_in_dim.70), calls=%async_computation.3 | async-start | bytes 8192 | tf_op jit(solution)/shard_map/all_to_all | solution.py:89

commit v2 on v1

v2 whole, which is shorter than its diff:
```python
import functools
import math

import jax
import jax.numpy as jnp
import numpy as np
from jax import lax
from jax.experimental import pallas as pl
from jax.experimental.pallas import tpu as pltpu
from jax.sharding import PartitionSpec as P

neg_large = -1e30

resp_parts = (("y_lo", 4), ("z", 8), ("core", 2))
mp_parts = (("y_hi", 2), ("x", 4))
resp_axes = tuple(name for name, _ in resp_parts)
mp_axes = tuple(name for name, _ in mp_parts)
axis_size = dict(resp_parts + mp_parts)


def gather_by_all_to_all(x, axes):
    count = int(np.prod([axis_size[a] for a in axes]))
    copies = jnp.broadcast_to(x[None], (count,) + x.shape)
    got = lax.all_to_all(copies, axes, 0, 0, tiled=True)
    return got.reshape((count * x.shape[0],) + x.shape[1:])


def attend_kernel(length_ref, q_ref, far_ref, near_ref, out_ref, *, factor):
    length = length_ref[0]
    tokens, head_size = q_ref.shape
    q = q_ref[...]
    contract = (((1,), (1,)), ((), ()))
    far = lax.dot_general(q, far_ref[:, :head_size], contract, preferred_element_type=jnp.float32) * factor
    near = lax.dot_general(q, near_ref[:, :head_size], contract, preferred_element_type=jnp.float32) * factor
    query_pos = lax.broadcasted_iota(jnp.int32, near.shape, 0)
    key_pos = lax.broadcasted_iota(jnp.int32, near.shape, 1)
    allowed = (key_pos <= query_pos) & (key_pos < length)
    near = jnp.where(allowed, near, neg_large)
    top = jnp.maximum(jnp.max(far, axis=1, keepdims=True), jnp.max(near, axis=1, keepdims=True))
    far_w = jnp.exp(far - top)
    near_w = jnp.where(allowed, jnp.exp(near - top), 0.0)
    total = jnp.sum(far_w, axis=1, keepdims=True) + jnp.sum(near_w, axis=1, keepdims=True)
    mixed = jnp.dot(far_w.astype(jnp.bfloat16), far_ref[:, head_size:], preferred_element_type=jnp.float32)
    mixed = mixed + jnp.dot(near_w.astype(jnp.bfloat16), near_ref[:, head_size:], preferred_element_type=jnp.float32)
    mixed = mixed / total
    live = lax.broadcasted_iota(jnp.int32, mixed.shape, 0) < length
    out_ref[...] = jnp.where(live, mixed, 0.0).astype(out_ref.dtype)


def attend(lengths, queries, far_kv, near_kv):
    tokens, heads, head_size = queries.shape
    flat = queries.reshape(tokens, heads * head_size)
    keys = far_kv.shape[0]
    kernel = functools.partial(attend_kernel, factor=1.0 / math.sqrt(head_size))
    return pl.pallas_call(
        kernel,
        grid=(heads,),
        in_specs=[
            pl.BlockSpec(memory_space=pltpu.SMEM),
            pl.BlockSpec((tokens, head_size), lambda h: (0, h)),
            pl.BlockSpec((keys, 2 * head_size), lambda h: (0, 0)),
            pl.BlockSpec((tokens, 2 * head_size), lambda h: (0, 0)),
        ],
        out_specs=pl.BlockSpec((tokens, head_size), lambda h: (0, h)),
        out_shape=jax.ShapeDtypeStruct((tokens, heads * head_size), jnp.bfloat16),
    )(lengths, flat, far_kv, near_kv)


def per_device(queries, response_kv, prefix_kv, lengths, score_weight):
    resp_len, local_heads, head_size = queries.shape
    length = lengths[0]
    mine = lax.all_to_all(prefix_kv, mp_axes, split_axis=2, concat_axis=0, tiled=True)
    collected = gather_by_all_to_all(gather_by_all_to_all(mine, ("y_lo", "z")), ("core",))
    far_kv = collected.reshape(collected.shape[0], 2 * head_size)
    near_kv = response_kv.reshape(resp_len, 2 * head_size)
    attended = attend(lengths, queries, far_kv, near_kv)
    partial_score = jnp.sum(attended.astype(jnp.float32) * score_weight[None, :])
    spread = jnp.broadcast_to(partial_score, (axis_size["y_hi"] * axis_size["x"],))
    summed = jnp.sum(lax.all_to_all(spread, mp_axes, 0, 0, tiled=True))
    score = (summed / length.astype(jnp.float32)).reshape(1)
    return (attended, score)


def solution(mesh):
    sizes = tuple(n for _, n in resp_parts) + tuple(n for _, n in mp_parts)
    fine = jax.sharding.Mesh(np.asarray(mesh.devices).reshape(sizes), resp_axes + mp_axes)
    R, M = resp_axes, mp_axes
    in_specs = (
        P(R, M, None),
        P(R, None, M, None),
        P(R + M, None, None, None),
        P(R),
        P(M),
    )
    out_specs = (P(R, M), P(R))
    return jax.shard_map(
        per_device, mesh=fine, in_specs=in_specs, out_specs=out_specs, check_vma=False
    )
```

time: 116 us -> 109 us (0.940)
  the two profiles are of different devices: /device:TPU:16 before, /device:TPU:64 now
where the time goes in v2:
time: 109 us; the launch traced here: 108 us
  waiting for transfers between devices  34.7 us (32%)
  blocking collectives  24.9 us (23%)
  Pallas kernels  21 us (19%)
  starting transfers between devices  13.7 us (13%)
  local copies, waits for them, and re-layouts  8.34 us (8%)
  between operations  3.12 us (3%)
  other arithmetic  2.53 us (2%)
    all_to_all x1, waiting for transfers between devices, gather_by_all_to_all(): got = lax.all_to_all(copies, axes, 0, 0, tiled=True)  24.6 us
    pallas_call x1, Pallas kernels, attend(): pl.pallas_call(kernel, grid=(heads,), in_specs=[pl.BlockSpec(memory_space...  21 us
    all_to_all x1, blocking collectives, per_device(): lax.all_to_all(prefix_kv, mp_axes, split_axis=2, concat_axis=0, tiled=True)  19.5 us
    all_to_all x1, starting transfers between devices, gather_by_all_to_all(): got = lax.all_to_all(copies, axes, 0, 0, tiled=True)  10.5 us
    all_to_all x1, waiting for transfers between devices, per_device(): summed = jnp.sum(lax.all_to_all(spread, mp_axes, 0, 0, tiled=True))  10 us
    all_to_all x1, blocking collectives, gather_by_all_to_all(): got = lax.all_to_all(copies, axes, 0, 0, tiled=True)  5.42 us
    unnamed x10, local copies, waits for them, and re-layouts  4.01 us
    all_to_all x1, starting transfers between devices, per_device(): summed = jnp.sum(lax.all_to_all(spread, mp_axes, 0, 0, tiled=True))  3.28 us
  transfers between devices with their start and end apart: 2, of which 2 were waited for; matrix products, arithmetic and copies ran while one was open for 1% of the time, Pallas kernels for 0%

profile of v2, /device:TPU:64, one launch (start us, length us, event | category | flops | bytes accessed | tf_op | source)
XLA Modules:
  0.0 108.4 jit_solution(7861022615431045937)
XLA Ops:
  0.6 0.0 copy-start
  0.6 0.8 copy.15
  1.5 19.5 %all_to_all.31 = bf16[8,2,8,128]{3,0,1,2:T(8,128)(2,1)S(1)} all-to-all(bf16[8,2,8,128]{3,0,1,2:T(8,128)(2,1)S(1)} %copy.15), channel_id=1, replica_groups=mesh['y_lo'=4,'z'=8,'core'=2,'y_hi'=2,'x'=4] {'y_hi','x'}, dimensions={2} | all-to-all | bytes 65536 | tf_op jit(solution)/shard_map/all_to_all | solution.py:72
  21.0 0.0 copy-start.1
  21.0 1.9 %broadcast_in_dim.20 = bf16[32,64,2,1,128]{4,2,1,3,0:T(2,128)(2,1)} broadcast(bf16[64,2,128]{2,1,0:T(2,128)(2,1)S(1)} %copy.17), dimensions={1,2,4} | broadcast | bytes 1081344 | tf_op jit(solution)/shard_map/broadcast_in_dim | solution.py:23
  23.0 10.5 %all-to-all-start.1 = ((bf16[32,64,2,1,128]{4,2,1,3,0:T(2,128)(2,1)}), bf16[32,64,2,1,128]{4,2,1,3,0:T(2,128)(2,1)S(1)}, u32[]{:S(2)}, u32[]{:S(2)}) async-start(bf16[32,64,2,1,128]{4,2,1,3,0:T(2,128)(2,1)} %broadcast_in_dim.20), calls=%async_computation.1 | async-start | bytes 2097152 | tf_op jit(solution)/shard_map/all_to_all | solution.py:24
  34.1 0.0 copy-done
  34.1 0.9 copy.28
  35.0 0.0 copy-done.1
  35.0 0.7 copy.29
  35.7 24.6 %all-to-all-done.1 = bf16[32,64,2,1,128]{4,2,1,3,0:T(2,128)(2,1)S(1)} async-done(((bf16[32,64,2,1,128]{4,2,1,3,0:T(2,128)(2,1)}), bf16[32,64,2,1,128]{4,2,1,3,0:T(2,128)(2,1)S(1)}, u32[]{:S(2)}, u32[]{:S(2)}) %all-to-all-start.1) | async-done | bytes 1048608 | tf_op jit(solution)/shard_map/all_to_all | solution.py:24
  60.3 1.1 %broadcast_in_dim.22 = bf16[2,2048,2,1,128]{4,2,1,3,0:T(2,128)(2,1)S(1)} broadcast(bf16[2048,2,128]{2,1,0:T(2,128)(2,1)S(1)} %bitcast.28), dimensions={1,2,4} | broadcast | bytes 3145728 | tf_op jit(solution)/shard_map/broadcast_in_dim | solution.py:23
  61.4 5.4 %all_to_all.32 = bf16[2,2048,2,1,128]{4,2,1,3,0:T(2,128)(2,1)S(1)} all-to-all(bf16[2,2048,2,1,128]{4,2,1,3,0:T(2,128)(2,1)S(1)} %broadcast_in_dim.22), channel_id=1, replica_groups=mesh['y_lo'=4,'z'=8,'core'=2,'y_hi'=2,'x'=4] {'core'}, dimensions={0} | all-to-all | bytes 4194304 | tf_op jit(solution)/shard_map/all_to_all | solution.py:24
  66.9 1.6 %copy.27 = bf16[512,8,2,128]{3,1,2,0:T(8,128)(2,1)} copy(bf16[512,8,2,128]{3,2,1,0:T(2,128)(2,1)S(1)} %bitcast.27) | data formatting | bytes 4194304
  68.5 0.0 copy-start.2
  68.5 21.0 %shard_map.68 = bf16[256,1024]{1,0:T(8,128)(2,1)} custom-call(s32[1]{0:T(128)S(6)} %copy.31.length_ref, bf16[256,1024]{1,0:T(8,128)(2,1)} %bitcast.29, bf16[4096,256]{1,0:T(8,128)(2,1)} %bitcast.26, bf16[256,256]{1,0:T(8,128)(2,1)} %bitcast.30), custom_call_target="tpu_custom_call" | custom-call | tf_op jit(solution)/shard_map/pallas_call | solution.py:55
  89.5 0.0 copy-done.2
  89.5 1.9 %multiply_reduce_fusion = f32[]{:T(128)} fusion(bf16[256,1024]{1,0:T(8,128)(2,1)} %shard_map.68, f32[1024]{0:T(1024)S(1)} %copy-done.2), kind=kLoop, calls=%fused_computation.1 | loop fusion | flops 786431 | bytes 528388 | tf_op jit(solution)/shard_map/reduce_sum | solution.py:77
  91.4 1.2 %broadcast_in_dim.23 = f32[8,1,1]{2,1,0:T(1,128)} broadcast(f32[]{:T(128)} %multiply_reduce_fusion), dimensions={} | broadcast | bytes 36 | tf_op jit(solution)/shard_map/broadcast_in_dim | solution.py:78
  92.7 3.3 %all-to-all-start.3 = ((f32[8,1,1]{2,1,0:T(1,128)}), f32[8,1,1]{2,1,0:T(1,128)S(1)}, u32[]{:S(2)}, u32[]{:S(2)}) async-start(f32[8,1,1]{2,1,0:T(1,128)} %broadcast_in_dim.23), calls=%async_computation.3 | async-start | bytes 8192 | tf_op jit(solution)/shard_map/all_to_all | solution.py:79
  96.0 10.0 %all-to-all-done.3 = f32[8,1,1]{2,1,0:T(1,128)S(1)} async-done(((f32[8,1,1]{2,1,0:T(1,128)}), f32[8,1,1]{2,1,0:T(1,128)S(1)}, u32[]{:S(2)}, u32[]{:S(2)}) %all-to-all-start.3) | async-done | bytes 64 | tf_op jit(solution)/shard_map/all_to_all | solution.py:79
  106.0 0.6 reduce_sum.19
  (2 shorter events, 0.0 us)
Async XLA Ops:
  0.6 33.5 %copy-start = (bf16[256,8,128]{2,1,0:T(8,128)(2,1)S(1)}, bf16[256,8,128]{2,1,0:T(8,128)(2,1)}, u32[]{:S(2)}) copy-start(bf16[256,8,128]{2,1,0:T(8,128)(2,1)} %param.5) | copy-start | bytes 1572868
  21.0 14.0 %copy-start.1 = (bf16[256,2,1,128]{3,1,2,0:T(2,128)(2,1)S(1)}, bf16[256,2,1,128]{3,1,2,0:T(2,128)(2,1)}, u32[]{:S(2)}) copy-start(bf16[256,2,1,128]{3,1,2,0:T(2,128)(2,1)} %param.6) | copy-start | bytes 393220
  23.0 37.3 %all-to-all-start.1 = ((bf16[32,64,2,1,128]{4,2,1,3,0:T(2,128)(2,1)}), bf16[32,64,2,1,128]{4,2,1,3,0:T(2,128)(2,1)S(1)}, u32[]{:S(2)}, u32[]{:S(2)}) async-start(bf16[32,64,2,1,128]{4,2,1,3,0:T(2,128)(2,1)} %broadcast_in_dim.20), calls=%async_computation.1 | async-start | bytes 2097152 | tf_op jit(solution)/shard_map/all_to_all | solution.py:24
  68.5 21.1 %copy-start.2 = (f32[1024]{0:T(1024)S(1)}, f32[1024]{0:T(1024)}, u32[]{:S(2)}) copy-start(f32[1024]{0:T(1024)} %param.9) | copy-start | bytes 12292
  92.7 13.3 %all-to-all-start.3 = ((f32[8,1,1]{2,1,0:T(1,128)}), f32[8,1,1]{2,1,0:T(1,128)S(1)}, u32[]{:S(2)}, u32[]{:S(2)}) async-start(f32[8,1,1]{2,1,0:T(1,128)} %broadcast_in_dim.23), calls=%async_computation.3 | async-start | bytes 8192 | tf_op jit(solution)/shard_map/all_to_all | solution.py:79

commit v3 on v2

v3 whole, which is shorter than its diff:
```python
import functools
import math

import jax
import jax.numpy as jnp
import numpy as np
from jax import lax
from jax.experimental import pallas as pl
from jax.experimental.pallas import tpu as pltpu
from jax.sharding import PartitionSpec as P

neg_large = -1e30

resp_parts = (("y_lo", 4), ("z", 8), ("core", 2))
mp_parts = (("y_hi", 2), ("x", 4))
resp_axes = tuple(name for name, _ in resp_parts)
mp_axes = tuple(name for name, _ in mp_parts)
axis_size = dict(resp_parts + mp_parts)


def gather_by_all_to_all(x, axes):
    count = int(np.prod([axis_size[a] for a in axes]))
    copies = jnp.broadcast_to(x[None], (count,) + x.shape)
    got = lax.all_to_all(copies, axes, 0, 0, tiled=True)
    return got.reshape((count * x.shape[0],) + x.shape[1:])


def attend_kernel(length_ref, q_ref, far_keys_ref, far_values_ref, near_keys_ref, near_values_ref, weight_ref, out_ref, part_ref, *, factor):
    length = length_ref[0]
    q = q_ref[...]
    far = jnp.dot(q, far_keys_ref[...], preferred_element_type=jnp.float32) * factor
    near = jnp.dot(q, near_keys_ref[...], preferred_element_type=jnp.float32) * factor
    query_pos = lax.broadcasted_iota(jnp.int32, near.shape, 0)
    key_pos = lax.broadcasted_iota(jnp.int32, near.shape, 1)
    allowed = (key_pos <= query_pos) & (key_pos < length)
    near = jnp.where(allowed, near, neg_large)
    top = jnp.maximum(jnp.max(far, axis=1, keepdims=True), jnp.max(near, axis=1, keepdims=True))
    far_w = jnp.exp(far - top)
    near_w = jnp.where(allowed, jnp.exp(near - top), 0.0)
    total = jnp.sum(far_w, axis=1, keepdims=True) + jnp.sum(near_w, axis=1, keepdims=True)
    mixed = jnp.dot(far_w.astype(jnp.bfloat16), far_values_ref[...], preferred_element_type=jnp.float32)
    mixed = mixed + jnp.dot(near_w.astype(jnp.bfloat16), near_values_ref[...], preferred_element_type=jnp.float32)
    mixed = mixed / total
    live = lax.broadcasted_iota(jnp.int32, mixed.shape, 0) < length
    rounded = jnp.where(live, mixed, 0.0).astype(out_ref.dtype)
    out_ref[...] = rounded
    weighted = rounded.astype(jnp.float32) * weight_ref[...]
    rows, lanes = weighted.shape
    part_ref[...] = jnp.sum(weighted.reshape(rows // 8, 8, lanes), axis=0)[None]


def attend(lengths, queries, far_keys_t, far_values, near_keys_t, near_values, score_weight):
    tokens, heads, head_size = queries.shape
    flat = queries.reshape(tokens, heads * head_size)
    keys = far_values.shape[0]
    kernel = functools.partial(attend_kernel, factor=1.0 / math.sqrt(head_size))
    whole = lambda h: (0, 0)
    return pl.pallas_call(
        kernel,
        grid=(heads,),
        in_specs=[
            pl.BlockSpec(memory_space=pltpu.SMEM),
            pl.BlockSpec((tokens, head_size), lambda h: (0, h)),
            pl.BlockSpec((head_size, keys), whole),
            pl.BlockSpec((keys, head_size), whole),
            pl.BlockSpec((head_size, tokens), whole),
            pl.BlockSpec((tokens, head_size), whole),
            pl.BlockSpec((1, head_size), lambda h: (0, h)),
        ],
        out_specs=[
            pl.BlockSpec((tokens, head_size), lambda h: (0, h)),
            pl.BlockSpec((1, 8, head_size), lambda h: (h, 0, 0)),
        ],
        out_shape=[
            jax.ShapeDtypeStruct((tokens, heads * head_size), jnp.bfloat16),
            jax.ShapeDtypeStruct((heads, 8, head_size), jnp.float32),
        ],
    )(lengths, flat, far_keys_t, far_values, near_keys_t, near_values, score_weight.reshape(1, -1))


def per_device(queries, response_kv, prefix_kv, lengths, score_weight):
    resp_len, local_heads, head_size = queries.shape
    length = lengths[0]
    spread_axes = ("y_lo", "z") + mp_axes
    groups = int(np.prod([axis_size[a] for a in ("y_lo", "z")]))
    by_head = jnp.transpose(prefix_kv, (2, 0, 1, 3))
    pieces = jnp.broadcast_to(by_head[None], (groups,) + by_head.shape)
    pieces = pieces.reshape((groups * by_head.shape[0],) + by_head.shape[1:])
    half = lax.all_to_all(pieces, spread_axes, 0, 0, tiled=True)
    half = half.reshape((-1,) + half.shape[2:])
    collected = gather_by_all_to_all(half, ("core",))
    far_keys_t = collected[:, 0].T
    far_values = collected[:, 1]
    near_keys_t = response_kv[:, 0, 0].T
    near_values = response_kv[:, 1, 0]
    attended, parts = attend(lengths, queries, far_keys_t, far_values, near_keys_t, near_values, score_weight)
    partial_score = jnp.sum(parts)
    spread = jnp.broadcast_to(partial_score, (axis_size["y_hi"] * axis_size["x"],))
    summed = jnp.sum(lax.all_to_all(spread, mp_axes, 0, 0, tiled=True))
    score = (summed / length.astype(jnp.float32)).reshape(1)
    return (attended, score)


def solution(mesh):
    sizes = tuple(n for _, n in resp_parts) + tuple(n for _, n in mp_parts)
    fine = jax.sharding.Mesh(np.asarray(mesh.devices).reshape(sizes), resp_axes + mp_axes)
    R, M = resp_axes, mp_axes
    in_specs = (
        P(R, M, None),
        P(R, None, M, None),
        P(R + M, None, None, None),
        P(R),
        P(M),
    )
    out_specs = (P(R, M), P(R))
    return jax.shard_map(
        per_device, mesh=fine, in_specs=in_specs, out_specs=out_specs, check_vma=False
    )
```

time: 109 us -> 105 us (0.963)
  the two profiles are of different devices: /device:TPU:64 before, /device:TPU:16 now
where the time goes in v3:
time: 105 us; the launch traced here: 104 us
  waiting for transfers between devices  37.3 us (36%)
  starting transfers between devices  27 us (26%)
  Pallas kernels  20.9 us (20%)
  local copies, waits for them, and re-layouts  8.63 us (8%)
  blocking collectives  5.42 us (5%)
  between operations  3.14 us (3%)
  other arithmetic  1.98 us (2%)
    all_to_all x1, waiting for transfers between devices, per_device(): half = lax.all_to_all(pieces, spread_axes, 0, 0, tiled=True)  27.2 us
    all_to_all x1, starting transfers between devices, per_device(): half = lax.all_to_all(pieces, spread_axes, 0, 0, tiled=True)  22 us
    pallas_call x1, Pallas kernels, attend(): pl.pallas_call(kernel, grid=(heads,), in_specs=[pl.BlockSpec(memory_space...  20.9 us
    all_to_all x1, waiting for transfers between devices, per_device(): summed = jnp.sum(lax.all_to_all(spread, mp_axes, 0, 0, tiled=True))  10.1 us
    all_to_all x1, blocking collectives, gather_by_all_to_all(): got = lax.all_to_all(copies, axes, 0, 0, tiled=True)  5.42 us
    all_to_all x1, starting transfers between devices, per_device(): summed = jnp.sum(lax.all_to_all(spread, mp_axes, 0, 0, tiled=True))  5.01 us
    unnamed x7, local copies, waits for them, and re-layouts  2.26 us
  transfers between devices with their start and end apart: 2, of which 2 were waited for; matrix products, arithmetic and copies ran while one was open for 2% of the time, Pallas kernels for 0%

profile of v3, /device:TPU:16, one launch (start us, length us, event | category | flops | bytes accessed | tf_op | source)
XLA Modules:
  0.0 104.4 jit_solution(13093043695624917595)
XLA Ops:
  0.6 0.0 copy-start.1
  0.6 0.0 copy-start
  0.6 0.8 copy.28
  1.5 1.2 %broadcast_in_dim.16 = bf16[32,8,8,2,128]{4,2,3,1,0:T(8,128)(2,1)} broadcast(bf16[8,8,2,128]{3,1,2,0:T(8,128)(2,1)S(1)} %copy.28), dimensions={1,2,3,4} | broadcast | bytes 1081344 | tf_op jit(solution)/shard_map/broadcast_in_dim | solution.py:87
  2.7 22.0 %all-to-all-start = ((bf16[256,8,2,128]{3,1,2,0:T(8,128)(2,1)}), bf16[256,8,2,128]{3,1,2,0:T(8,128)(2,1)S(1)}, u32[]{:S(2)}, u32[]{:S(2)}) async-start(bf16[256,8,2,128]{3,1,2,0:T(8,128)(2,1)} %bitcast.1), calls=%async_computation | async-start | bytes 2097152 | tf_op jit(solution)/shard_map/all_to_all | solution.py:89
  24.7 0.0 copy-done.1
  24.7 0.2 fusion
  24.9 0.6 copy.44
  25.5 0.7 copy.36
  26.9 0.0 copy-done
  26.9 0.9 copy.43
  27.8 27.2 %all-to-all-done = bf16[256,8,2,128]{3,1,2,0:T(8,128)(2,1)S(1)} async-done(((bf16[256,8,2,128]{3,1,2,0:T(8,128)(2,1)}), bf16[256,8,2,128]{3,1,2,0:T(8,128)(2,1)S(1)}, u32[]{:S(2)}, u32[]{:S(2)}) %all-to-all-start) | async-done | bytes 1048608 | tf_op jit(solution)/shard_map/all_to_all | solution.py:89
  55.0 0.1 copy.42
  55.1 0.3 broadcast_in_dim.18
  55.4 5.4 %all_to_all.16 = bf16[2,2048,2,128]{3,1,2,0:T(8,128)(2,1)S(1)} all-to-all(bf16[2,2048,2,128]{3,1,2,0:T(8,128)(2,1)S(1)} %broadcast_in_dim.18), channel_id=1, replica_groups=mesh['y_lo'=4,'z'=8,'core'=2,'y_hi'=2,'x'=4] {'core'}, dimensions={0} | all-to-all | bytes 4194304 | tf_op jit(solution)/shard_map/all_to_all | solution.py:24
  60.8 0.1 copy.30
  61.0 1.1 %slice_bitcast_fusion = (bf16[4096,128]{1,0:T(8,128)(2,1)}, bf16[128,4096]{0,1:T(8,128)(2,1)S(1)}) fusion(bf16[4096,2,128]{2,0,1:T(8,128)(2,1)S(1)} %bitcast.25), kind=kLoop, calls=%fused_computation | loop fusion | bytes 4194304 | tf_op jit(solution)/shard_map/squeeze | solution.py:93
  62.1 1.3 %copy.33.far_keys_ref = bf16[128,4096]{1,0:T(8,128)(2,1)} copy(bf16[128,4096]{0,1:T(8,128)(2,1)S(1)} %get-tuple-element.7) | data formatting | bytes 2097152 | tf_op jit(solution)/shard_map/transpose | solution.py:92
  63.4 20.9 %shard_map.68 = (bf16[256,1024]{1,0:T(8,128)(2,1)}, f32[8,8,128]{2,1,0:T(8,128)}) custom-call(s32[1]{0:T(128)S(6)} %copy.45.length_ref, bf16[256,1024]{1,0:T(8,128)(2,1)} %bitcast.27, bf16[128,4096]{1,0:T(8,128)(2,1)} %copy.33.far_keys_ref, bf16[4096,128]{1,0:T(8,128)(2,1)} %get-tuple-element.6.far_values_ref, bf16[128,256]{1,0:T(8,128)(2,1)} %bitcast.30, ...), custom_call_target="tpu_custom_call" | custom-call | tf_op jit(solution)/shard_map/pallas_call | solution.py:58
  84.3 1.4 %reduce_sum.18 = f32[]{:T(128)} reduce(f32[8,8,128]{2,1,0:T(8,128)} %get-tuple-element.5, f32[]{:T(128)} %constant.0.clone.1), dimensions={0,1,2}, to_apply=%region_0.0 | reduce | flops 8191 | bytes 32776 | tf_op jit(solution)/shard_map/reduce_sum | solution.py:97
  85.6 1.2 %broadcast_in_dim.19 = f32[8,1,1]{2,1,0:T(1,128)} broadcast(f32[]{:T(128)} %reduce_sum.18), dimensions={} | broadcast | bytes 36 | tf_op jit(solution)/shard_map/broadcast_in_dim | solution.py:98
  86.9 5.0 %all-to-all-start.2 = ((f32[8,1,1]{2,1,0:T(1,128)}), f32[8,1,1]{2,1,0:T(1,128)S(1)}, u32[]{:S(2)}, u32[]{:S(2)}) async-start(f32[8,1,1]{2,1,0:T(1,128)} %broadcast_in_dim.19), calls=%async_computation.2 | async-start | bytes 8192 | tf_op jit(solution)/shard_map/all_to_all | solution.py:99
  91.9 10.1 %all-to-all-done.2 = f32[8,1,1]{2,1,0:T(1,128)S(1)} async-done(((f32[8,1,1]{2,1,0:T(1,128)}), f32[8,1,1]{2,1,0:T(1,128)S(1)}, u32[]{:S(2)}, u32[]{:S(2)}) %all-to-all-start.2) | async-done | bytes 64 | tf_op jit(solution)/shard_map/all_to_all | solution.py:99
  102.0 0.6 reduce_sum.19
Async XLA Ops:
  0.6 24.0 %copy-start.1 = (bf16[256,2,1,128]{3,1,2,0:T(2,128)(2,1)S(1)}, bf16[256,2,1,128]{3,1,2,0:T(2,128)(2,1)}, u32[]{:S(2)}) copy-start(bf16[256,2,1,128]{3,1,2,0:T(2,128)(2,1)} %param.6) | copy-start | bytes 393220
  0.6 26.2 %copy-start = (bf16[256,8,128]{2,1,0:T(8,128)(2,1)S(1)}, bf16[256,8,128]{2,1,0:T(8,128)(2,1)}, u32[]{:S(2)}) copy-start(bf16[256,8,128]{2,1,0:T(8,128)(2,1)} %param.5) | copy-start | bytes 1572868
  2.7 52.4 %all-to-all-start = ((bf16[256,8,2,128]{3,1,2,0:T(8,128)(2,1)}), bf16[256,8,2,128]{3,1,2,0:T(8,128)(2,1)S(1)}, u32[]{:S(2)}, u32[]{:S(2)}) async-start(bf16[256,8,2,128]{3,1,2,0:T(8,128)(2,1)} %bitcast.1), calls=%async_computation | async-start | bytes 2097152 | tf_op jit(solution)/shard_map/all_to_all | solution.py:89
  86.9 15.1 %all-to-all-start.2 = ((f32[8,1,1]{2,1,0:T(1,128)}), f32[8,1,1]{2,1,0:T(1,128)S(1)}, u32[]{:S(2)}, u32[]{:S(2)}) async-start(f32[8,1,1]{2,1,0:T(1,128)} %broadcast_in_dim.19), calls=%async_computation.2 | async-start | bytes 8192 | tf_op jit(solution)/shard_map/all_to_all | solution.py:99

commit v4 on v3

v4 whole, which is shorter than its diff:
```python
import functools
import math

import jax
import jax.numpy as jnp
import numpy as np
from jax import lax
from jax.experimental import pallas as pl
from jax.experimental.pallas import tpu as pltpu
from jax.sharding import PartitionSpec as P

neg_large = -1e30

resp_parts = (("y_lo", 4), ("z", 8), ("core", 2))
mp_parts = (("y_hi", 2), ("x", 4))
resp_axes = tuple(name for name, _ in resp_parts)
mp_axes = tuple(name for name, _ in mp_parts)
axis_size = dict(resp_parts + mp_parts)


def gather_by_all_to_all(x, axes):
    count = int(np.prod([axis_size[a] for a in axes]))
    copies = jnp.broadcast_to(x[None], (count,) + x.shape)
    got = lax.all_to_all(copies, axes, 0, 0, tiled=True)
    return got.reshape((count * x.shape[0],) + x.shape[1:])


def attend_kernel(length_ref, q_ref, far_keys_ref, far_values_ref, near_keys_ref, near_values_ref, weight_ref, out_ref, part_ref, *, factor, chunk):
    head, block = pl.program_id(0), pl.program_id(1)
    length = length_ref[0]
    rows, head_size = q_ref.shape
    steps = far_values_ref.shape[0] // chunk
    q = q_ref[...]
    near = jnp.dot(q, near_keys_ref[...], preferred_element_type=jnp.float32)
    query_pos = lax.broadcasted_iota(jnp.int32, near.shape, 0) + block * rows
    key_pos = lax.broadcasted_iota(jnp.int32, near.shape, 1)
    allowed = (key_pos <= query_pos) & (key_pos < length)

    def far_scores(c):
        start = pl.multiple_of(c * chunk, chunk)
        return jnp.dot(q, far_keys_ref[:, pl.ds(start, chunk)], preferred_element_type=jnp.float32), start

    def widest(c, best):
        scores, _ = far_scores(c)
        return jnp.maximum(best, scores)

    best = lax.fori_loop(0, steps, widest, jnp.full((rows, chunk), neg_large, jnp.float32))
    top = jnp.maximum(jnp.max(best, axis=1, keepdims=True), jnp.max(jnp.where(allowed, near, neg_large), axis=1, keepdims=True)) * factor

    def absorb(c, carry):
        sums, accum = carry
        scores, start = far_scores(c)
        weights = jnp.exp(scores * factor - top)
        accum = accum + jnp.dot(weights.astype(jnp.bfloat16), far_values_ref[pl.ds(start, chunk), :], preferred_element_type=jnp.float32)
        return sums + weights, accum

    zeros = jnp.zeros((rows, chunk), jnp.float32)
    sums, accum = lax.fori_loop(0, steps, absorb, (zeros, jnp.zeros((rows, head_size), jnp.float32)))
    near_w = jnp.where(allowed, jnp.exp(near * factor - top), 0.0)
    total = jnp.sum(sums, axis=1, keepdims=True) + jnp.sum(near_w, axis=1, keepdims=True)
    accum = accum + jnp.dot(near_w.astype(jnp.bfloat16), near_values_ref[...], preferred_element_type=jnp.float32)
    mixed = accum / total
    live = lax.broadcasted_iota(jnp.int32, mixed.shape, 0) + block * rows < length
    rounded = jnp.where(live, mixed, 0.0).astype(out_ref.dtype)
    out_ref[...] = rounded
    weighted = rounded.astype(jnp.float32) * weight_ref[...]
    folded = jnp.sum(weighted.reshape(rows // 8, 8, head_size), axis=0)

    @pl.when((head == 0) & (block == 0))
    def _():
        part_ref[...] = jnp.zeros_like(part_ref)

    part_ref[...] += folded

    @pl.when((head == pl.num_programs(0) - 1) & (block == pl.num_programs(1) - 1))
    def _():
        part_ref[...] = jnp.broadcast_to(jnp.sum(part_ref[...]), part_ref.shape)


def attend(lengths, queries, far_keys_t, far_values, near_keys_t, near_values, score_weight, copies):
    tokens, heads, head_size = queries.shape
    flat = queries.reshape(tokens, heads * head_size)
    keys = far_values.shape[0]
    rows = 128
    kernel = functools.partial(attend_kernel, factor=1.0 / math.sqrt(head_size), chunk=128)
    whole = lambda h, b: (0, 0)
    return pl.pallas_call(
        kernel,
        grid=(heads, tokens // rows),
        in_specs=[
            pl.BlockSpec(memory_space=pltpu.SMEM),
            pl.BlockSpec((rows, head_size), lambda h, b: (b, h)),
            pl.BlockSpec((head_size, keys), whole),
            pl.BlockSpec((keys, head_size), whole),
            pl.BlockSpec((head_size, tokens), whole),
            pl.BlockSpec((tokens, head_size), whole),
            pl.BlockSpec((1, head_size), lambda h, b: (0, h)),
        ],
        out_specs=[
            pl.BlockSpec((rows, head_size), lambda h, b: (b, h)),
            pl.BlockSpec((copies, head_size), whole),
        ],
        out_shape=[
            jax.ShapeDtypeStruct((tokens, heads * head_size), jnp.bfloat16),
            jax.ShapeDtypeStruct((copies, head_size), jnp.float32),
        ],
    )(lengths, flat, far_keys_t, far_values, near_keys_t, near_values, score_weight.reshape(1, -1))


def per_device(queries, response_kv, prefix_kv, lengths, score_weight):
    resp_len, local_heads, head_size = queries.shape
    length = lengths[0]
    spread_axes = ("y_lo", "z") + mp_axes
    groups = int(np.prod([axis_size[a] for a in ("y_lo", "z")]))
    by_head = jnp.transpose(prefix_kv, (2, 0, 1, 3))
    pieces = jnp.broadcast_to(by_head[None], (groups,) + by_head.shape)
    pieces = pieces.reshape((groups * by_head.shape[0],) + by_head.shape[1:])
    half = lax.all_to_all(pieces, spread_axes, 0, 0, tiled=True)
    half = half.reshape((-1,) + half.shape[2:])
    collected = gather_by_all_to_all(half, ("core",))
    far_keys_t = collected[:, 0].T
    far_values = collected[:, 1]
    near_keys_t = response_kv[:, 0, 0].T
    near_values = response_kv[:, 1, 0]
    copies = axis_size["y_hi"] * axis_size["x"]
    attended, spread = attend(lengths, queries, far_keys_t, far_values, near_keys_t, near_values, score_weight, copies)
    summed = jnp.sum(lax.all_to_all(spread, mp_axes, 0, 0, tiled=True)[:, 0])
    score = (summed / length.astype(jnp.float32)).reshape(1)
    return (attended, score)


def solution(mesh):
    sizes = tuple(n for _, n in resp_parts) + tuple(n for _, n in mp_parts)
    fine = jax.sharding.Mesh(np.asarray(mesh.devices).reshape(sizes), resp_axes + mp_axes)
    R, M = resp_axes, mp_axes
    in_specs = (
        P(R, M, None),
        P(R, None, M, None),
        P(R + M, None, None, None),
        P(R),
        P(M),
    )
    out_specs = (P(R, M), P(R))
    return jax.shard_map(
        per_device, mesh=fine, in_specs=in_specs, out_specs=out_specs, check_vma=False
    )
```

time: 105 us -> 305 us (2.90)
  Pallas kernels: 20.9 us -> 224 us
    pallas_call x1, Pallas kernels: 20.9 us -> 224 us  [attend(): pl.pallas_call(kernel, grid=(heads, tokens // rows), in_specs=[pl.BlockSp...]
  transfers between devices with their start and end apart: 2 -> 2, of which waited for: 2 -> 2; matrix products, arithmetic and copies ran while one was open for 2% -> 1% of each run, Pallas kernels for 0% -> 0%
where the time goes in v4:
time: 305 us
  Pallas kernels  224 us (73%)
  waiting for transfers between devices  37.3 us (12%)
  starting transfers between devices  27 us (9%)
  local copies, waits for them, and re-layouts  7.45 us (2%)
  blocking collectives  5.42 us (2%)
  between operations  3.14 us (1%)
    pallas_call x1, Pallas kernels, attend(): pl.pallas_call(kernel, grid=(heads, tokens // rows), in_specs=[pl.BlockSp...  224 us
    all_to_all x1, waiting for transfers between devices, per_device(): half = lax.all_to_all(pieces, spread_axes, 0, 0, tiled=True)  27.2 us
    all_to_all x1, starting transfers between devices, per_device(): half = lax.all_to_all(pieces, spread_axes, 0, 0, tiled=True)  22 us
    all_to_all x1, waiting for transfers between devices, per_device(): summed = jnp.sum(lax.all_to_all(spread, mp_axes, 0, 0, tiled=True)[:, 0])  10.1 us
  transfers between devices with their start and end apart: 2, of which 2 were waited for; matrix products, arithmetic and copies ran while one was open for 1% of the time, Pallas kernels for 0%

profile of v4, /device:TPU:16, one launch (start us, length us, event | category | flops | bytes accessed | tf_op | source)
XLA Modules:
  0.0 304.9 jit_solution(2886271072686489634)
XLA Ops:
  0.6 0.0 copy-start.1
  0.6 0.0 copy-start
  0.6 0.8 copy.17
  1.5 1.2 broadcast_in_dim.6
  2.7 22.0 %all-to-all-start = ((bf16[256,8,2,128]{3,1,2,0:T(8,128)(2,1)}), bf16[256,8,2,128]{3,1,2,0:T(8,128)(2,1)S(1)}, u32[]{:S(2)}, u32[]{:S(2)}) async-start(bf16[256,8,2,128]{3,1,2,0:T(8,128)(2,1)} %bitcast.1), calls=%async_computation | async-start | bytes 2097152 | tf_op jit(solution)/shard_map/all_to_all | solution.py:118
  24.7 0.0 copy-done.1
  24.7 0.2 fusion
  24.9 0.6 copy.32
  25.5 0.7 copy.24
  26.9 0.0 copy-done
  26.9 0.9 copy.31
  27.8 27.2 %all-to-all-done = bf16[256,8,2,128]{3,1,2,0:T(8,128)(2,1)S(1)} async-done(((bf16[256,8,2,128]{3,1,2,0:T(8,128)(2,1)}), bf16[256,8,2,128]{3,1,2,0:T(8,128)(2,1)S(1)}, u32[]{:S(2)}, u32[]{:S(2)}) %all-to-all-start) | async-done | bytes 1048608 | tf_op jit(solution)/shard_map/all_to_all | solution.py:118
  55.0 0.1 copy.30
  55.1 0.3 broadcast_in_dim.15
  55.4 5.4 %all_to_all.22 = bf16[2,2048,2,128]{3,1,2,0:T(8,128)(2,1)S(1)} all-to-all(bf16[2,2048,2,128]{3,1,2,0:T(8,128)(2,1)S(1)} %broadcast_in_dim.15), channel_id=1, replica_groups=mesh['y_lo'=4,'z'=8,'core'=2,'y_hi'=2,'x'=4] {'core'}, dimensions={0} | all-to-all | bytes 4194304 | tf_op jit(solution)/shard_map/all_to_all | solution.py:24
  60.8 0.1 copy.19
  61.0 1.1 slice_bitcast_fusion
  62.1 1.3 copy.22.far_keys_ref
  63.4 224.1 %shard_map.68 = (bf16[256,1024]{1,0:T(8,128)(2,1)}, f32[8,128]{1,0:T(8,128)}) custom-call(s32[1]{0:T(128)S(6)} %copy.33.length_ref, bf16[256,1024]{1,0:T(8,128)(2,1)} %bitcast.31, bf16[128,4096]{1,0:T(8,128)(2,1)} %copy.22.far_keys_ref, bf16[4096,128]{1,0:T(8,128)(2,1)} %get-tuple-element.6.far_values_ref, bf16[128,256]{1,0:T(8,128)(2,1)} %bitcast.34, ...), custom_call_target="tpu_custom_call" | custom-call | tf_op jit(solution)/shard_map/pallas_call | solution.py:87
  287.5 5.0 %all-to-all-start.2 = ((f32[8,1,128]{2,1,0:T(1,128)}), f32[8,1,128]{2,1,0:T(1,128)S(1)}, u32[]{:S(2)}, u32[]{:S(2)}) async-start(f32[8,1,128]{2,1,0:T(1,128)} %bitcast.38), calls=%async_computation.2 | async-start | bytes 8192 | tf_op jit(solution)/shard_map/all_to_all | solution.py:127
  292.5 10.1 %all-to-all-done.2 = f32[8,1,128]{2,1,0:T(1,128)S(1)} async-done(((f32[8,1,128]{2,1,0:T(1,128)}), f32[8,1,128]{2,1,0:T(1,128)S(1)}, u32[]{:S(2)}, u32[]{:S(2)}) %all-to-all-start.2) | async-done | bytes 4128 | tf_op jit(solution)/shard_map/all_to_all | solution.py:127
  302.6 0.6 slice_reduce_fusion
Async XLA Ops:
  0.6 24.0 %copy-start.1 = (bf16[256,2,1,128]{3,1,2,0:T(2,128)(2,1)S(1)}, bf16[256,2,1,128]{3,1,2,0:T(2,128)(2,1)}, u32[]{:S(2)}) copy-start(bf16[256,2,1,128]{3,1,2,0:T(2,128)(2,1)} %param.6) | copy-start | bytes 393220
  0.6 26.3 %copy-start = (bf16[256,8,128]{2,1,0:T(8,128)(2,1)S(1)}, bf16[256,8,128]{2,1,0:T(8,128)(2,1)}, u32[]{:S(2)}) copy-start(bf16[256,8,128]{2,1,0:T(8,128)(2,1)} %param.5) | copy-start | bytes 1572868
  2.7 52.4 %all-to-all-start = ((bf16[256,8,2,128]{3,1,2,0:T(8,128)(2,1)}), bf16[256,8,2,128]{3,1,2,0:T(8,128)(2,1)S(1)}, u32[]{:S(2)}, u32[]{:S(2)}) async-start(bf16[256,8,2,128]{3,1,2,0:T(8,128)(2,1)} %bitcast.1), calls=%async_computation | async-start | bytes 2097152 | tf_op jit(solution)/shard_map/all_to_all | solution.py:118
  287.5 15.1 %all-to-all-start.2 = ((f32[8,1,128]{2,1,0:T(1,128)}), f32[8,1,128]{2,1,0:T(1,128)S(1)}, u32[]{:S(2)}, u32[]{:S(2)}) async-start(f32[8,1,128]{2,1,0:T(1,128)} %bitcast.38), calls=%async_computation.2 | async-start | bytes 8192 | tf_op jit(solution)/shard_map/all_to_all | solution.py:127

commit v5 on v3

--- a/solution.py
+++ b/solution.py
@@ -26,6 +26,7 @@
 
 
 def attend_kernel(length_ref, q_ref, far_keys_ref, far_values_ref, near_keys_ref, near_values_ref, weight_ref, out_ref, part_ref, *, factor):
+    head = pl.program_id(0)
     length = length_ref[0]
     q = q_ref[...]
     far = jnp.dot(q, far_keys_ref[...], preferred_element_type=jnp.float32) * factor
@@ -46,10 +47,20 @@
     out_ref[...] = rounded
     weighted = rounded.astype(jnp.float32) * weight_ref[...]
     rows, lanes = weighted.shape
-    part_ref[...] = jnp.sum(weighted.reshape(rows // 8, 8, lanes), axis=0)[None]
+    folded = jnp.sum(weighted.reshape(rows // 8, 8, lanes), axis=0)
+
+    @pl.when(head == 0)
+    def _():
+        part_ref[...] = jnp.zeros_like(part_ref)
+
+    part_ref[...] += folded
+
+    @pl.when(head == pl.num_programs(0) - 1)
+    def _():
+        part_ref[...] = jnp.broadcast_to(jnp.sum(part_ref[...]), part_ref.shape)
 
 
-def attend(lengths, queries, far_keys_t, far_values, near_keys_t, near_values, score_weight):
+def attend(lengths, queries, far_keys_t, far_values, near_keys_t, near_values, score_weight, copies):
     tokens, heads, head_size = queries.shape
     flat = queries.reshape(tokens, heads * head_size)
     keys = far_values.shape[0]
@@ -69,11 +80,11 @@
         ],
         out_specs=[
             pl.BlockSpec((tokens, head_size), lambda h: (0, h)),
-            pl.BlockSpec((1, 8, head_size), lambda h: (h, 0, 0)),
+            pl.BlockSpec((copies, head_size), whole),
         ],
         out_shape=[
             jax.ShapeDtypeStruct((tokens, heads * head_size), jnp.bfloat16),
-            jax.ShapeDtypeStruct((heads, 8, head_size), jnp.float32),
+            jax.ShapeDtypeStruct((copies, head_size), jnp.float32),
         ],
     )(lengths, flat, far_keys_t, far_values, near_keys_t, near_values, score_weight.reshape(1, -1))
 
@@ -93,10 +104,9 @@
     far_values = collected[:, 1]
     near_keys_t = response_kv[:, 0, 0].T
     near_values = response_kv[:, 1, 0]
-    attended, parts = attend(lengths, queries, far_keys_t, far_values, near_keys_t, near_values, score_weight)
-    partial_score = jnp.sum(parts)
-    spread = jnp.broadcast_to(partial_score, (axis_size["y_hi"] * axis_size["x"],))
-    summed = jnp.sum(lax.all_to_all(spread, mp_axes, 0, 0, tiled=True))
+    copies = axis_size["y_hi"] * axis_size["x"]
+    attended, spread = attend(lengths, queries, far_keys_t, far_values, near_keys_t, near_values, score_weight, copies)
+    summed = jnp.sum(lax.all_to_all(spread, mp_axes, 0, 0, tiled=True)[:, 0])
     score = (summed / length.astype(jnp.float32)).reshape(1)
     return (attended, score)
 

time: 105 us -> 102 us (0.971)
  other arithmetic: 1.98 us -> 0.6 us
  local copies, waits for them, and re-layouts: 8.63 us -> 7.45 us
    reduce_sum x2 -> x1, other arithmetic: 1.98 us -> 0.6 us  [per_device(): summed = jnp.sum(lax.all_to_all(spread, mp_axes, 0, 0, tiled=True)[:, 0])]
    broadcast_in_dim x1 -> x0, local copies, waits for them, and re-layouts: 1.24 us -> none  [per_device(): jnp.broadcast_to(partial_score, (axis_size['y_hi'] * axis_size['x'],))]
where the time goes in v5:
time: 102 us
  waiting for transfers between devices  37.3 us (37%)
  starting transfers between devices  27 us (26%)
  Pallas kernels  21 us (21%)
  local copies, waits for them, and re-layouts  7.45 us (7%)
  blocking collectives  5.42 us (5%)
  between operations  3.14 us (3%)
    all_to_all x1, waiting for transfers between devices, per_device(): half = lax.all_to_all(pieces, spread_axes, 0, 0, tiled=True)  27.2 us
    all_to_all x1, starting transfers between devices, per_device(): half = lax.all_to_all(pieces, spread_axes, 0, 0, tiled=True)  22 us
    pallas_call x1, Pallas kernels, attend(): pl.pallas_call(kernel, grid=(heads,), in_specs=[pl.BlockSpec(memory_space...  21 us
    all_to_all x1, waiting for transfers between devices, per_device(): summed = jnp.sum(lax.all_to_all(spread, mp_axes, 0, 0, tiled=True)[:, 0])  10.1 us
    all_to_all x1, blocking collectives, gather_by_all_to_all(): got = lax.all_to_all(copies, axes, 0, 0, tiled=True)  5.42 us
    all_to_all x1, starting transfers between devices, per_device(): summed = jnp.sum(lax.all_to_all(spread, mp_axes, 0, 0, tiled=True)[:, 0])  5.01 us
    unnamed x7, local copies, waits for them, and re-layouts  2.3 us
  transfers between devices with their start and end apart: 2, of which 2 were waited for; matrix products, arithmetic and copies ran while one was open for 2% of the time, Pallas kernels for 0%

profile of v5, /device:TPU:16, one launch (start us, length us, event | category | flops | bytes accessed | tf_op | source)
XLA Modules:
  0.0 101.9 jit_solution(131942694630703766)
XLA Ops:
  0.6 0.0 copy-start.1
  0.6 0.0 copy-start
  0.6 0.8 copy.17
  1.5 1.2 %broadcast_in_dim.6 = bf16[32,8,8,2,128]{4,2,3,1,0:T(8,128)(2,1)} broadcast(bf16[8,8,2,128]{3,1,2,0:T(8,128)(2,1)S(1)} %copy.17), dimensions={1,2,3,4} | broadcast | bytes 1081344 | tf_op jit(solution)/shard_map/broadcast_in_dim | solution.py:98
  2.7 22.0 %all-to-all-start = ((bf16[256,8,2,128]{3,1,2,0:T(8,128)(2,1)}), bf16[256,8,2,128]{3,1,2,0:T(8,128)(2,1)S(1)}, u32[]{:S(2)}, u32[]{:S(2)}) async-start(bf16[256,8,2,128]{3,1,2,0:T(8,128)(2,1)} %bitcast.1), calls=%async_computation | async-start | bytes 2097152 | tf_op jit(solution)/shard_map/all_to_all | solution.py:100
  24.7 0.0 copy-done.1
  24.7 0.2 fusion
  24.9 0.6 copy.32
  25.5 0.7 copy.24
  26.9 0.0 copy-done
  26.9 0.9 copy.31
  27.8 27.2 %all-to-all-done = bf16[256,8,2,128]{3,1,2,0:T(8,128)(2,1)S(1)} async-done(((bf16[256,8,2,128]{3,1,2,0:T(8,128)(2,1)}), bf16[256,8,2,128]{3,1,2,0:T(8,128)(2,1)S(1)}, u32[]{:S(2)}, u32[]{:S(2)}) %all-to-all-start) | async-done | bytes 1048608 | tf_op jit(solution)/shard_map/all_to_all | solution.py:100
  55.0 0.1 copy.30
  55.1 0.3 broadcast_in_dim.15
  55.4 5.4 %all_to_all.22 = bf16[2,2048,2,128]{3,1,2,0:T(8,128)(2,1)S(1)} all-to-all(bf16[2,2048,2,128]{3,1,2,0:T(8,128)(2,1)S(1)} %broadcast_in_dim.15), channel_id=1, replica_groups=mesh['y_lo'=4,'z'=8,'core'=2,'y_hi'=2,'x'=4] {'core'}, dimensions={0} | all-to-all | bytes 4194304 | tf_op jit(solution)/shard_map/all_to_all | solution.py:24
  60.8 0.1 copy.19
  61.0 1.1 %slice_bitcast_fusion = (bf16[4096,128]{1,0:T(8,128)(2,1)}, bf16[128,4096]{0,1:T(8,128)(2,1)S(1)}) fusion(bf16[4096,2,128]{2,0,1:T(8,128)(2,1)S(1)} %bitcast.29), kind=kLoop, calls=%fused_computation | loop fusion | bytes 4194304 | tf_op jit(solution)/shard_map/squeeze | solution.py:104
  62.1 1.3 %copy.22.far_keys_ref = bf16[128,4096]{1,0:T(8,128)(2,1)} copy(bf16[128,4096]{0,1:T(8,128)(2,1)S(1)} %get-tuple-element.7) | data formatting | bytes 2097152 | tf_op jit(solution)/shard_map/transpose | solution.py:103
  63.4 21.0 %shard_map.68 = (bf16[256,1024]{1,0:T(8,128)(2,1)}, f32[8,128]{1,0:T(8,128)}) custom-call(s32[1]{0:T(128)S(6)} %copy.33.length_ref, bf16[256,1024]{1,0:T(8,128)(2,1)} %bitcast.31, bf16[128,4096]{1,0:T(8,128)(2,1)} %copy.22.far_keys_ref, bf16[4096,128]{1,0:T(8,128)(2,1)} %get-tuple-element.6.far_values_ref, bf16[128,256]{1,0:T(8,128)(2,1)} %bitcast.34, ...), custom_call_target="tpu_custom_call" | custom-call | tf_op jit(solution)/shard_map/pallas_call | solution.py:69
  84.4 5.0 %all-to-all-start.2 = ((f32[8,1,128]{2,1,0:T(1,128)}), f32[8,1,128]{2,1,0:T(1,128)S(1)}, u32[]{:S(2)}, u32[]{:S(2)}) async-start(f32[8,1,128]{2,1,0:T(1,128)} %bitcast.38), calls=%async_computation.2 | async-start | bytes 8192 | tf_op jit(solution)/shard_map/all_to_all | solution.py:109
  89.4 10.1 %all-to-all-done.2 = f32[8,1,128]{2,1,0:T(1,128)S(1)} async-done(((f32[8,1,128]{2,1,0:T(1,128)}), f32[8,1,128]{2,1,0:T(1,128)S(1)}, u32[]{:S(2)}, u32[]{:S(2)}) %all-to-all-start.2) | async-done | bytes 4128 | tf_op jit(solution)/shard_map/all_to_all | solution.py:109
  99.5 0.6 slice_reduce_fusion
Async XLA Ops:
  0.6 24.0 %copy-start.1 = (bf16[256,2,1,128]{3,1,2,0:T(2,128)(2,1)S(1)}, bf16[256,2,1,128]{3,1,2,0:T(2,128)(2,1)}, u32[]{:S(2)}) copy-start(bf16[256,2,1,128]{3,1,2,0:T(2,128)(2,1)} %param.6) | copy-start | bytes 393220
  0.6 26.3 %copy-start = (bf16[256,8,128]{2,1,0:T(8,128)(2,1)S(1)}, bf16[256,8,128]{2,1,0:T(8,128)(2,1)}, u32[]{:S(2)}) copy-start(bf16[256,8,128]{2,1,0:T(8,128)(2,1)} %param.5) | copy-start | bytes 1572868
  2.7 52.4 %all-to-all-start = ((bf16[256,8,2,128]{3,1,2,0:T(8,128)(2,1)}), bf16[256,8,2,128]{3,1,2,0:T(8,128)(2,1)S(1)}, u32[]{:S(2)}, u32[]{:S(2)}) async-start(bf16[256,8,2,128]{3,1,2,0:T(8,128)(2,1)} %bitcast.1), calls=%async_computation | async-start | bytes 2097152 | tf_op jit(solution)/shard_map/all_to_all | solution.py:100
  84.4 15.1 %all-to-all-start.2 = ((f32[8,1,128]{2,1,0:T(1,128)}), f32[8,1,128]{2,1,0:T(1,128)S(1)}, u32[]{:S(2)}, u32[]{:S(2)}) async-start(f32[8,1,128]{2,1,0:T(1,128)} %bitcast.38), calls=%async_computation.2 | async-start | bytes 8192 | tf_op jit(solution)/shard_map/all_to_all | solution.py:109

commit v6 on v5

--- a/solution.py
+++ b/solution.py
@@ -8,6 +8,7 @@
 from jax.experimental import pallas as pl
 from jax.experimental.pallas import tpu as pltpu
 from jax.sharding import PartitionSpec as P
+
 
 neg_large = -1e30
 
@@ -25,8 +26,7 @@
     return got.reshape((count * x.shape[0],) + x.shape[1:])
 
 
-def attend_kernel(length_ref, q_ref, far_keys_ref, far_values_ref, near_keys_ref, near_values_ref, weight_ref, out_ref, part_ref, *, factor):
-    head = pl.program_id(0)
+def first_kernel(length_ref, q_ref, far_keys_ref, far_values_ref, near_keys_ref, near_values_ref, top_ref, total_ref, accum_ref, *, factor):
     length = length_ref[0]
     q = q_ref[...]
     far = jnp.dot(q, far_keys_ref[...], preferred_element_type=jnp.float32) * factor
@@ -41,6 +41,22 @@
     total = jnp.sum(far_w, axis=1, keepdims=True) + jnp.sum(near_w, axis=1, keepdims=True)
     mixed = jnp.dot(far_w.astype(jnp.bfloat16), far_values_ref[...], preferred_element_type=jnp.float32)
     mixed = mixed + jnp.dot(near_w.astype(jnp.bfloat16), near_values_ref[...], preferred_element_type=jnp.float32)
+    top_ref[...] = jnp.broadcast_to(top, top_ref.shape)
+    total_ref[...] = jnp.broadcast_to(total, total_ref.shape)
+    accum_ref[...] = mixed
+
+
+def second_kernel(length_ref, q_ref, far_keys_ref, far_values_ref, top_ref, total_ref, accum_ref, weight_ref, out_ref, part_ref, *, factor):
+    head = pl.program_id(0)
+    length = length_ref[0]
+    q = q_ref[...]
+    far = jnp.dot(q, far_keys_ref[...], preferred_element_type=jnp.float32) * factor
+    before = top_ref[:, :1]
+    top = jnp.maximum(before, jnp.max(far, axis=1, keepdims=True))
+    shrink = jnp.exp(before - top)
+    far_w = jnp.exp(far - top)
+    total = total_ref[:, :1] * shrink + jnp.sum(far_w, axis=1, keepdims=True)
+    mixed = accum_ref[...] * shrink + jnp.dot(far_w.astype(jnp.bfloat16), far_values_ref[...], preferred_element_type=jnp.float32)
     mixed = mixed / total
     live = lax.broadcasted_iota(jnp.int32, mixed.shape, 0) < length
     rounded = jnp.where(live, mixed, 0.0).astype(out_ref.dtype)
@@ -60,52 +76,82 @@
         part_ref[...] = jnp.broadcast_to(jnp.sum(part_ref[...]), part_ref.shape)
 
 
-def attend(lengths, queries, far_keys_t, far_values, near_keys_t, near_values, score_weight, copies):
-    tokens, heads, head_size = queries.shape
-    flat = queries.reshape(tokens, heads * head_size)
+def attend_first(lengths, flat, far_keys_t, far_values, near_keys_t, near_values, head_size):
+    tokens = flat.shape[0]
+    heads = flat.shape[1] // head_size
     keys = far_values.shape[0]
-    kernel = functools.partial(attend_kernel, factor=1.0 / math.sqrt(head_size))
+    kernel = functools.partial(first_kernel, factor=1.0 / math.sqrt(head_size))
     whole = lambda h: (0, 0)
+    per_head = pl.BlockSpec((tokens, head_size), lambda h: (0, h))
+    state = jax.ShapeDtypeStruct((tokens, heads * head_size), jnp.float32)
     return pl.pallas_call(
         kernel,
         grid=(heads,),
         in_specs=[
             pl.BlockSpec(memory_space=pltpu.SMEM),
-            pl.BlockSpec((tokens, head_size), lambda h: (0, h)),
+            per_head,
             pl.BlockSpec((head_size, keys), whole),
             pl.BlockSpec((keys, head_size), whole),
             pl.BlockSpec((head_size, tokens), whole),
             pl.BlockSpec((tokens, head_size), whole),
+        ],
+        out_specs=[per_head, per_head, per_head],
+        out_shape=[state, state, state],
+    )(lengths, flat, far_keys_t, far_values, near_keys_t, near_values)
+
+
+def attend_second(lengths, flat, far_keys_t, far_values, top, total, accum, score_weight, head_size, copies):
+    tokens = flat.shape[0]
+    heads = flat.shape[1] // head_size
+    keys = far_values.shape[0]
+    kernel = functools.partial(second_kernel, factor=1.0 / math.sqrt(head_size))
+    whole = lambda h: (0, 0)
+    per_head = pl.BlockSpec((tokens, head_size), lambda h: (0, h))
+    return pl.pallas_call(
+        kernel,
+        grid=(heads,),
+        in_specs=[
+            pl.BlockSpec(memory_space=pltpu.SMEM),
+            per_head,
+            pl.BlockSpec((head_size, keys), whole),
+            pl.BlockSpec((keys, head_size), whole),
+            per_head,
+            per_head,
+            per_head,
             pl.BlockSpec((1, head_size), lambda h: (0, h)),
         ],
-        out_specs=[
-            pl.BlockSpec((tokens, head_size), lambda h: (0, h)),
-            pl.BlockSpec((copies, head_size), whole),
-        ],
+        out_specs=[per_head, pl.BlockSpec((copies, head_size), whole)],
         out_shape=[
             jax.ShapeDtypeStruct((tokens, heads * head_size), jnp.bfloat16),
             jax.ShapeDtypeStruct((copies, head_size), jnp.float32),
         ],
-    )(lengths, flat, far_keys_t, far_values, near_keys_t, near_values, score_weight.reshape(1, -1))
+    )(lengths, flat, far_keys_t, far_values, top, total, accum, score_weight.reshape(1, -1))
 
 
-def per_device(queries, response_kv, prefix_kv, lengths, score_weight):
-    resp_len, local_heads, head_size = queries.shape
-    length = lengths[0]
+def fetch_prompt(by_head):
     spread_axes = ("y_lo", "z") + mp_axes
     groups = int(np.prod([axis_size[a] for a in ("y_lo", "z")]))
-    by_head = jnp.transpose(prefix_kv, (2, 0, 1, 3))
     pieces = jnp.broadcast_to(by_head[None], (groups,) + by_head.shape)
     pieces = pieces.reshape((groups * by_head.shape[0],) + by_head.shape[1:])
     half = lax.all_to_all(pieces, spread_axes, 0, 0, tiled=True)
     half = half.reshape((-1,) + half.shape[2:])
     collected = gather_by_all_to_all(half, ("core",))
-    far_keys_t = collected[:, 0].T
-    far_values = collected[:, 1]
+    return collected[:, 0].T, collected[:, 1]
+
+
+def per_device_body(queries, response_kv, prefix_kv, lengths, score_weight):
+    resp_len, local_heads, head_size = queries.shape
+    length = lengths[0]
+    by_head = jnp.transpose(prefix_kv, (2, 0, 1, 3))
+    split = by_head.shape[1] // 2
+    keys_a, values_a = fetch_prompt(by_head[:, :split])
+    keys_b, values_b = fetch_prompt(by_head[:, split:])
+    flat = queries.reshape(resp_len, local_heads * head_size)
     near_keys_t = response_kv[:, 0, 0].T
     near_values = response_kv[:, 1, 0]
+    top, total, accum = attend_first(lengths, flat, keys_a, values_a, near_keys_t, near_values, head_size)
     copies = axis_size["y_hi"] * axis_size["x"]
-    attended, spread = attend(lengths, queries, far_keys_t, far_values, near_keys_t, near_values, score_weight, copies)
+    attended, spread = attend_second(lengths, flat, keys_b, values_b, top, total, accum, score_weight, head_size, copies)
     summed = jnp.sum(lax.all_to_all(spread, mp_axes, 0, 0, tiled=True)[:, 0])
     score = (summed / length.astype(jnp.float32)).reshape(1)
     return (attended, score)
@@ -123,6 +169,4 @@
         P(M),
     )
     out_specs = (P(R, M), P(R))
-    return jax.shard_map(
-        per_device, mesh=fine, in_specs=in_specs, out_specs=out_specs, check_vma=False
-    )
+    return jax.shard_map(per_device_body, mesh=fine, in_specs=in_specs, out_specs=out_specs, check_vma=False)

time: 102 us -> 130 us (1.27)
  starting transfers between devices: 27 us -> 35.7 us
  waiting for transfers between devices: 37.3 us -> 45.2 us
  Pallas kernels: 21 us -> 25.4 us
  blocking collectives: 5.42 us -> 9.15 us
  local copies, waits for them, and re-layouts: 7.45 us -> 9.86 us
    all_to_all x2 -> x3, starting transfers between devices: 27 us -> 35.7 us  [the longest x2 31.3 us: fetch_prompt(): half = lax.all_to_all(pieces, spread_axes, 0, 0, tiled=True)]
    all_to_all x2 -> x3, waiting for transfers between devices: 37.3 us -> 45.2 us  [the longest x2 35.1 us: fetch_prompt(): half = lax.all_to_all(pieces, spread_axes, 0, 0, tiled=True)]
    pallas_call x1 -> x2, Pallas kernels: 21 us -> 25.4 us  [the longest x1 12.8 us: attend_second(): pl.pallas_call(kernel, grid=(heads,), in_specs=[pl.BlockSpec(memory_space...]
    all_to_all x1 -> x2, blocking collectives: 5.42 us -> 9.15 us  [gather_by_all_to_all(): got = lax.all_to_all(copies, axes, 0, 0, tiled=True)]
  transfers between devices with their start and end apart: 2 -> 3, of which waited for: 2 -> 3; matrix products, arithmetic and copies ran while one was open for 2% -> 3% of each run, Pallas kernels for 0% -> 0%
where the time goes in v6:
time: 130 us; the launch traced here: 129 us
  waiting for transfers between devices  45.2 us (35%)
  starting transfers between devices  35.7 us (27%)
  Pallas kernels  25.4 us (20%)
  local copies, waits for them, and re-layouts  9.86 us (8%)
  blocking collectives  9.15 us (7%)
  between operations  3.15 us (2%)
    all_to_all x2, waiting for transfers between devices, fetch_prompt(): half = lax.all_to_all(pieces, spread_axes, 0, 0, tiled=True)  35.1 us
    all_to_all x2, starting transfers between devices, fetch_prompt(): half = lax.all_to_all(pieces, spread_axes, 0, 0, tiled=True)  31.3 us
    pallas_call x1, Pallas kernels, attend_second(): pl.pallas_call(kernel, grid=(heads,), in_specs=[pl.BlockSpec(memory_space...  12.8 us
    pallas_call x1, Pallas kernels, attend_first(): pl.pallas_call(kernel, grid=(heads,), in_specs=[pl.BlockSpec(memory_space...  12.6 us
    all_to_all x1, waiting for transfers between devices, per_device_body(): summed = jnp.sum(lax.all_to_all(spread, mp_axes, 0, 0, tiled=True)[:, 0])  10.1 us
    all_to_all x2, blocking collectives, gather_by_all_to_all(): got = lax.all_to_all(copies, axes, 0, 0, tiled=True)  9.15 us
    all_to_all x1, starting transfers between devices, per_device_body(): summed = jnp.sum(lax.all_to_all(spread, mp_axes, 0, 0, tiled=True)[:, 0])  4.41 us
  transfers between devices with their start and end apart: 3, of which 3 were waited for; matrix products, arithmetic and copies ran while one was open for 3% of the time, Pallas kernels for 0%

profile of v6, /device:TPU:16, one launch (start us, length us, event | category | flops | bytes accessed | tf_op | source)
XLA Modules:
  0.0 129.1 jit_solution(8607821651684675083)
XLA Ops:
  0.6 0.7 fusion.1
  1.4 1.0 broadcast_in_dim.29
  2.4 22.0 %all-to-all-start.2 = ((bf16[256,4,2,128]{3,1,2,0:T(4,128)(2,1)}), bf16[256,4,2,128]{3,1,2,0:T(4,128)(2,1)S(1)}, u32[]{:S(2)}, u32[]{:S(2)}) async-start(bf16[256,4,2,128]{3,1,2,0:T(4,128)(2,1)} %bitcast.7), calls=%async_computation.2 | async-start | bytes 1048576 | tf_op jit(solution)/shard_map/all_to_all | solution.py:136
  24.4 19.8 %all-to-all-done.2 = bf16[256,4,2,128]{3,1,2,0:T(4,128)(2,1)S(1)} async-done(((bf16[256,4,2,128]{3,1,2,0:T(4,128)(2,1)}), bf16[256,4,2,128]{3,1,2,0:T(4,128)(2,1)S(1)}, u32[]{:S(2)}, u32[]{:S(2)}) %all-to-all-start.2) | async-done | bytes 524320 | tf_op jit(solution)/shard_map/all_to_all | solution.py:136
  44.2 0.2 copy.26
  44.4 0.1 broadcast_in_dim.31
  44.6 4.6 %all_to_all.32 = bf16[2,1024,2,128]{3,1,2,0:T(8,128)(2,1)S(1)} all-to-all(bf16[2,1024,2,128]{3,1,2,0:T(8,128)(2,1)S(1)} %broadcast_in_dim.31), channel_id=1, replica_groups=mesh['y_lo'=4,'z'=8,'core'=2,'y_hi'=2,'x'=4] {'core'}, dimensions={0} | all-to-all | bytes 2097152 | tf_op jit(solution)/shard_map/all_to_all | solution.py:25
  49.2 1.0 broadcast_in_dim.12
  50.2 0.0 copy-start
  50.2 9.4 %all-to-all-start = ((bf16[256,4,2,128]{3,1,2,0:T(4,128)(2,1)}), bf16[256,4,2,128]{3,1,2,0:T(4,128)(2,1)S(1)}, u32[]{:S(2)}, u32[]{:S(2)}) async-start(bf16[256,4,2,128]{3,1,2,0:T(4,128)(2,1)} %bitcast.1), calls=%async_computation | async-start | bytes 1048576 | tf_op jit(solution)/shard_map/all_to_all | solution.py:136
  60.2 0.0 copy-done
  60.2 0.0 copy-start.1
  60.2 0.9 copy.38
  61.1 0.0 copy-done.1
  61.1 0.2 fusion
  61.3 0.7 copy.33
  62.1 0.6 copy.39
  62.7 0.1 copy.27
  62.8 0.9 slice_bitcast_fusion
  63.6 1.0 copy.30.far_keys_ref
  64.7 15.2 %all-to-all-done = bf16[256,4,2,128]{3,1,2,0:T(4,128)(2,1)S(1)} async-done(((bf16[256,4,2,128]{3,1,2,0:T(4,128)(2,1)}), bf16[256,4,2,128]{3,1,2,0:T(4,128)(2,1)S(1)}, u32[]{:S(2)}, u32[]{:S(2)}) %all-to-all-start) | async-done | bytes 524320 | tf_op jit(solution)/shard_map/all_to_all | solution.py:136
  79.9 0.2 copy.23
  80.1 0.1 broadcast_in_dim.28
  80.3 4.6 %all_to_all.33 = bf16[2,1024,2,128]{3,1,2,0:T(8,128)(2,1)S(1)} all-to-all(bf16[2,1024,2,128]{3,1,2,0:T(8,128)(2,1)S(1)} %broadcast_in_dim.28), channel_id=1, replica_groups=mesh['y_lo'=4,'z'=8,'core'=2,'y_hi'=2,'x'=4] {'core'}, dimensions={0} | all-to-all | bytes 2097152 | tf_op jit(solution)/shard_map/all_to_all | solution.py:25
  84.8 0.1 copy.24
  84.9 0.9 slice_bitcast_fusion.2
  85.8 1.0 copy.31.far_keys_ref
  86.8 12.6 %shard_map.68 = (f32[256,1024]{1,0:T(8,128)}, f32[256,1024]{1,0:T(8,128)}, f32[256,1024]{1,0:T(8,128)}) custom-call(s32[1]{0:T(128)S(6)} %copy.40.length_ref, bf16[256,1024]{1,0:T(8,128)(2,1)} %bitcast.36, bf16[128,2048]{1,0:T(8,128)(2,1)} %copy.30.far_keys_ref, bf16[2048,128]{1,0:T(8,128)(2,1)} %get-tuple-element.12.far_values_ref, ...), custom_call_target="tpu_custom_call" | custom-call | tf_op jit(solution)/shard_map/pallas_call | solution.py:87
  99.4 12.8 %shard_map.69 = (bf16[256,1024]{1,0:T(8,128)(2,1)}, f32[8,128]{1,0:T(8,128)}) custom-call(s32[1]{0:T(128)S(6)} %copy.40.length_ref, bf16[256,1024]{1,0:T(8,128)(2,1)} %bitcast.37, bf16[128,2048]{1,0:T(8,128)(2,1)} %copy.31.far_keys_ref, bf16[2048,128]{1,0:T(8,128)(2,1)} %get-tuple-element.14.far_values_ref, f32[256,1024]{1,0:T(8,128)} %get-tuple-element.7.top_ref, ...), custom_call_target="tpu_custom_call" | custom-call | tf_op jit(solution)/shard_map/pallas_call | solution.py:110
  112.2 4.4 %all-to-all-start.4 = ((f32[8,1,128]{2,1,0:T(1,128)}), f32[8,1,128]{2,1,0:T(1,128)S(1)}, u32[]{:S(2)}, u32[]{:S(2)}) async-start(f32[8,1,128]{2,1,0:T(1,128)} %bitcast.47), calls=%async_computation.4 | async-start | bytes 8192 | tf_op jit(solution)/shard_map/all_to_all | solution.py:155
  116.6 10.1 %all-to-all-done.4 = f32[8,1,128]{2,1,0:T(1,128)S(1)} async-done(((f32[8,1,128]{2,1,0:T(1,128)}), f32[8,1,128]{2,1,0:T(1,128)S(1)}, u32[]{:S(2)}, u32[]{:S(2)}) %all-to-all-start.4) | async-done | bytes 4128 | tf_op jit(solution)/shard_map/all_to_all | solution.py:155
  126.7 0.6 slice_reduce_fusion
  (2 shorter events, 0.0 us)
Async XLA Ops:
  2.4 41.8 %all-to-all-start.2 = ((bf16[256,4,2,128]{3,1,2,0:T(4,128)(2,1)}), bf16[256,4,2,128]{3,1,2,0:T(4,128)(2,1)S(1)}, u32[]{:S(2)}, u32[]{:S(2)}) async-start(bf16[256,4,2,128]{3,1,2,0:T(4,128)(2,1)} %bitcast.7), calls=%async_computation.2 | async-start | bytes 1048576 | tf_op jit(solution)/shard_map/all_to_all | solution.py:136
  50.2 10.0 %copy-start = (bf16[256,8,128]{2,1,0:T(8,128)(2,1)S(1)}, bf16[256,8,128]{2,1,0:T(8,128)(2,1)}, u32[]{:S(2)}) copy-start(bf16[256,8,128]{2,1,0:T(8,128)(2,1)} %param.5) | copy-start | bytes 1572868
  50.2 29.7 %all-to-all-start = ((bf16[256,4,2,128]{3,1,2,0:T(4,128)(2,1)}), bf16[256,4,2,128]{3,1,2,0:T(4,128)(2,1)S(1)}, u32[]{:S(2)}, u32[]{:S(2)}) async-start(bf16[256,4,2,128]{3,1,2,0:T(4,128)(2,1)} %bitcast.1), calls=%async_computation | async-start | bytes 1048576 | tf_op jit(solution)/shard_map/all_to_all | solution.py:136
  60.2 0.9 copy-start.1
  112.2 14.5 %all-to-all-start.4 = ((f32[8,1,128]{2,1,0:T(1,128)}), f32[8,1,128]{2,1,0:T(1,128)S(1)}, u32[]{:S(2)}, u32[]{:S(2)}) async-start(f32[8,1,128]{2,1,0:T(1,128)} %bitcast.47), calls=%async_computation.4 | async-start | bytes 8192 | tf_op jit(solution)/shard_map/all_to_all | solution.py:155

commit v7 on v5

--- a/solution.py
+++ b/solution.py
@@ -25,11 +25,13 @@
     return got.reshape((count * x.shape[0],) + x.shape[1:])
 
 
-def attend_kernel(length_ref, q_ref, far_keys_ref, far_values_ref, near_keys_ref, near_values_ref, weight_ref, out_ref, part_ref, *, factor):
+def attend_kernel(length_ref, q_ref, far_ref, near_keys_ref, near_values_ref, weight_ref, out_ref, part_ref, *, factor):
     head = pl.program_id(0)
     length = length_ref[0]
     q = q_ref[...]
-    far = jnp.dot(q, far_keys_ref[...], preferred_element_type=jnp.float32) * factor
+    head_size = q.shape[1]
+    contract = (((1,), (1,)), ((), ()))
+    far = lax.dot_general(q, far_ref[:, :head_size], contract, preferred_element_type=jnp.float32) * factor
     near = jnp.dot(q, near_keys_ref[...], preferred_element_type=jnp.float32) * factor
     query_pos = lax.broadcasted_iota(jnp.int32, near.shape, 0)
     key_pos = lax.broadcasted_iota(jnp.int32, near.shape, 1)
@@ -39,7 +41,7 @@
     far_w = jnp.exp(far - top)
     near_w = jnp.where(allowed, jnp.exp(near - top), 0.0)
     total = jnp.sum(far_w, axis=1, keepdims=True) + jnp.sum(near_w, axis=1, keepdims=True)
-    mixed = jnp.dot(far_w.astype(jnp.bfloat16), far_values_ref[...], preferred_element_type=jnp.float32)
+    mixed = jnp.dot(far_w.astype(jnp.bfloat16), far_ref[:, head_size:], preferred_element_type=jnp.float32)
     mixed = mixed + jnp.dot(near_w.astype(jnp.bfloat16), near_values_ref[...], preferred_element_type=jnp.float32)
     mixed = mixed / total
     live = lax.broadcasted_iota(jnp.int32, mixed.shape, 0) < length
@@ -60,10 +62,10 @@
         part_ref[...] = jnp.broadcast_to(jnp.sum(part_ref[...]), part_ref.shape)
 
 
-def attend(lengths, queries, far_keys_t, far_values, near_keys_t, near_values, score_weight, copies):
+def attend(lengths, queries, far_kv, near_keys_t, near_values, score_weight, copies):
     tokens, heads, head_size = queries.shape
     flat = queries.reshape(tokens, heads * head_size)
-    keys = far_values.shape[0]
+    keys = far_kv.shape[0]
     kernel = functools.partial(attend_kernel, factor=1.0 / math.sqrt(head_size))
     whole = lambda h: (0, 0)
     return pl.pallas_call(
@@ -72,8 +74,7 @@
         in_specs=[
             pl.BlockSpec(memory_space=pltpu.SMEM),
             pl.BlockSpec((tokens, head_size), lambda h: (0, h)),
-            pl.BlockSpec((head_size, keys), whole),
-            pl.BlockSpec((keys, head_size), whole),
+            pl.BlockSpec((keys, 2 * head_size), whole),
             pl.BlockSpec((head_size, tokens), whole),
             pl.BlockSpec((tokens, head_size), whole),
             pl.BlockSpec((1, head_size), lambda h: (0, h)),
@@ -86,7 +87,7 @@
             jax.ShapeDtypeStruct((tokens, heads * head_size), jnp.bfloat16),
             jax.ShapeDtypeStruct((copies, head_size), jnp.float32),
         ],
-    )(lengths, flat, far_keys_t, far_values, near_keys_t, near_values, score_weight.reshape(1, -1))
+    )(lengths, flat, far_kv, near_keys_t, near_values, score_weight.reshape(1, -1))
 
 
 def per_device(queries, response_kv, prefix_kv, lengths, score_weight):
@@ -100,12 +101,11 @@
     half = lax.all_to_all(pieces, spread_axes, 0, 0, tiled=True)
     half = half.reshape((-1,) + half.shape[2:])
     collected = gather_by_all_to_all(half, ("core",))
-    far_keys_t = collected[:, 0].T
-    far_values = collected[:, 1]
+    far_kv = collected.reshape(collected.shape[0], 2 * head_size)
     near_keys_t = response_kv[:, 0, 0].T
     near_values = response_kv[:, 1, 0]
     copies = axis_size["y_hi"] * axis_size["x"]
-    attended, spread = attend(lengths, queries, far_keys_t, far_values, near_keys_t, near_values, score_weight, copies)
+    attended, spread = attend(lengths, queries, far_kv, near_keys_t, near_values, score_weight, copies)
     summed = jnp.sum(lax.all_to_all(spread, mp_axes, 0, 0, tiled=True)[:, 0])
     score = (summed / length.astype(jnp.float32)).reshape(1)
     return (attended, score)

time: 102 us -> 103 us (level)
    unnamed x7 -> x8, local copies, waits for them, and re-layouts: 2.3 us -> 3.88 us
    transpose x1 -> x0, local copies, waits for them, and re-layouts: 1.34 us -> none  [per_device(): far_keys_t = collected[:, 0].T]
    squeeze x1 -> x0, local copies, waits for them, and re-layouts: 1.11 us -> none  [per_device(): far_values = collected[:, 1]]
where the time goes in v7:
time: 103 us
  waiting for transfers between devices  37.3 us (36%)
  starting transfers between devices  27 us (26%)
  Pallas kernels  21.5 us (21%)
  local copies, waits for them, and re-layouts  7.97 us (8%)
  blocking collectives  5.42 us (5%)
  between operations  3.13 us (3%)
    all_to_all x1, waiting for transfers between devices, per_device(): half = lax.all_to_all(pieces, spread_axes, 0, 0, tiled=True)  27.2 us
    all_to_all x1, starting transfers between devices, per_device(): half = lax.all_to_all(pieces, spread_axes, 0, 0, tiled=True)  22 us
    pallas_call x1, Pallas kernels, attend(): pl.pallas_call(kernel, grid=(heads,), in_specs=[pl.BlockSpec(memory_space...  21.5 us
    all_to_all x1, waiting for transfers between devices, per_device(): summed = jnp.sum(lax.all_to_all(spread, mp_axes, 0, 0, tiled=True)[:, 0])  10.1 us
    all_to_all x1, blocking collectives, gather_by_all_to_all(): got = lax.all_to_all(copies, axes, 0, 0, tiled=True)  5.42 us
    all_to_all x1, starting transfers between devices, per_device(): summed = jnp.sum(lax.all_to_all(spread, mp_axes, 0, 0, tiled=True)[:, 0])  5.01 us
    unnamed x8, local copies, waits for them, and re-layouts  3.88 us
  transfers between devices with their start and end apart: 2, of which 2 were waited for; matrix products, arithmetic and copies ran while one was open for 2% of the time, Pallas kernels for 0%

profile of v7, /device:TPU:16, one launch (start us, length us, event | category | flops | bytes accessed | tf_op | source)
XLA Modules:
  0.0 102.9 jit_solution(14883776590510330500)
XLA Ops:
  0.6 0.0 copy-start.1
  0.6 0.0 copy-start
  0.6 0.8 copy.10
  1.5 1.9 %broadcast_in_dim.6 = bf16[32,8,8,2,128]{4,3,2,1,0:T(2,128)(2,1)} broadcast(bf16[8,8,2,128]{3,2,1,0:T(2,128)(2,1)S(1)} %copy.10), dimensions={1,2,3,4} | broadcast | bytes 1081344 | tf_op jit(solution)/shard_map/broadcast_in_dim | solution.py:99
  3.4 22.0 %all-to-all-start = ((bf16[256,8,2,128]{3,2,1,0:T(2,128)(2,1)}), bf16[256,8,2,128]{3,2,1,0:T(2,128)(2,1)S(1)}, u32[]{:S(2)}, u32[]{:S(2)}) async-start(bf16[256,8,2,128]{3,2,1,0:T(2,128)(2,1)} %bitcast.1), calls=%async_computation | async-start | bytes 2097152 | tf_op jit(solution)/shard_map/all_to_all | solution.py:101
  25.4 0.0 copy-done.1
  25.4 0.2 fusion
  25.6 0.6 copy.23
  26.2 0.7 copy.14
  27.6 0.0 copy-done
  27.6 0.9 copy.22
  28.5 27.2 %all-to-all-done = bf16[256,8,2,128]{3,2,1,0:T(2,128)(2,1)S(1)} async-done(((bf16[256,8,2,128]{3,2,1,0:T(2,128)(2,1)}), bf16[256,8,2,128]{3,2,1,0:T(2,128)(2,1)S(1)}, u32[]{:S(2)}, u32[]{:S(2)}) %all-to-all-start) | async-done | bytes 1048608 | tf_op jit(solution)/shard_map/all_to_all | solution.py:101
  55.8 1.1 %broadcast_in_dim.15 = bf16[2,2048,2,128]{3,2,1,0:T(2,128)(2,1)S(1)} broadcast(bf16[2048,2,128]{2,1,0:T(2,128)(2,1)S(1)} %bitcast.27), dimensions={1,2,3} | broadcast | bytes 3145728 | tf_op jit(solution)/shard_map/broadcast_in_dim | solution.py:23
  56.9 5.4 %all_to_all.22 = bf16[2,2048,2,128]{3,2,1,0:T(2,128)(2,1)S(1)} all-to-all(bf16[2,2048,2,128]{3,2,1,0:T(2,128)(2,1)S(1)} %broadcast_in_dim.15), channel_id=1, replica_groups=mesh['y_lo'=4,'z'=8,'core'=2,'y_hi'=2,'x'=4] {'core'}, dimensions={0} | all-to-all | bytes 4194304 | tf_op jit(solution)/shard_map/all_to_all | solution.py:24
  62.3 1.6 %copy.21 = bf16[512,8,2,128]{3,1,2,0:T(8,128)(2,1)} copy(bf16[512,8,2,128]{3,2,1,0:T(2,128)(2,1)S(1)} %bitcast.26) | data formatting | bytes 4194304
  64.0 21.5 %shard_map.68 = (bf16[256,1024]{1,0:T(8,128)(2,1)}, f32[8,128]{1,0:T(8,128)}) custom-call(s32[1]{0:T(128)S(6)} %copy.24.length_ref, bf16[256,1024]{1,0:T(8,128)(2,1)} %bitcast.28, bf16[4096,256]{1,0:T(8,128)(2,1)} %bitcast.25, bf16[128,256]{1,0:T(8,128)(2,1)} %bitcast.31, bf16[256,128]{1,0:T(8,128)(2,1)} %bitcast.30, f32[1,1024]{1,0:T(1,128)} %bitcast.34), custom_call_target="tpu_custom_call" | custom-call | tf_op jit(solution)/shard_map/pallas_call | solution.py:71
  85.4 5.0 %all-to-all-start.2 = ((f32[8,1,128]{2,1,0:T(1,128)}), f32[8,1,128]{2,1,0:T(1,128)S(1)}, u32[]{:S(2)}, u32[]{:S(2)}) async-start(f32[8,1,128]{2,1,0:T(1,128)} %bitcast.35), calls=%async_computation.2 | async-start | bytes 8192 | tf_op jit(solution)/shard_map/all_to_all | solution.py:109
  90.5 10.1 %all-to-all-done.2 = f32[8,1,128]{2,1,0:T(1,128)S(1)} async-done(((f32[8,1,128]{2,1,0:T(1,128)}), f32[8,1,128]{2,1,0:T(1,128)S(1)}, u32[]{:S(2)}, u32[]{:S(2)}) %all-to-all-start.2) | async-done | bytes 4128 | tf_op jit(solution)/shard_map/all_to_all | solution.py:109
  100.5 0.6 slice_reduce_fusion
Async XLA Ops:
  0.6 24.8 %copy-start.1 = (bf16[256,2,1,128]{3,1,2,0:T(2,128)(2,1)S(1)}, bf16[256,2,1,128]{3,1,2,0:T(2,128)(2,1)}, u32[]{:S(2)}) copy-start(bf16[256,2,1,128]{3,1,2,0:T(2,128)(2,1)} %param.6) | copy-start | bytes 393220
  0.6 27.0 %copy-start = (bf16[256,8,128]{2,1,0:T(8,128)(2,1)S(1)}, bf16[256,8,128]{2,1,0:T(8,128)(2,1)}, u32[]{:S(2)}) copy-start(bf16[256,8,128]{2,1,0:T(8,128)(2,1)} %param.5) | copy-start | bytes 1572868
  3.4 52.4 %all-to-all-start = ((bf16[256,8,2,128]{3,2,1,0:T(2,128)(2,1)}), bf16[256,8,2,128]{3,2,1,0:T(2,128)(2,1)S(1)}, u32[]{:S(2)}, u32[]{:S(2)}) async-start(bf16[256,8,2,128]{3,2,1,0:T(2,128)(2,1)} %bitcast.1), calls=%async_computation | async-start | bytes 2097152 | tf_op jit(solution)/shard_map/all_to_all | solution.py:101
  85.4 15.1 %all-to-all-start.2 = ((f32[8,1,128]{2,1,0:T(1,128)}), f32[8,1,128]{2,1,0:T(1,128)S(1)}, u32[]{:S(2)}, u32[]{:S(2)}) async-start(f32[8,1,128]{2,1,0:T(1,128)} %bitcast.35), calls=%async_computation.2 | async-start | bytes 8192 | tf_op jit(solution)/shard_map/all_to_all | solution.py:109

commit v8 on v5

--- a/solution.py
+++ b/solution.py
@@ -92,10 +92,10 @@
 def per_device(queries, response_kv, prefix_kv, lengths, score_weight):
     resp_len, local_heads, head_size = queries.shape
     length = lengths[0]
-    spread_axes = ("y_lo", "z") + mp_axes
+    spread_axes = mp_axes + ("y_lo", "z")
     groups = int(np.prod([axis_size[a] for a in ("y_lo", "z")]))
     by_head = jnp.transpose(prefix_kv, (2, 0, 1, 3))
-    pieces = jnp.broadcast_to(by_head[None], (groups,) + by_head.shape)
+    pieces = jnp.broadcast_to(by_head[:, None], by_head.shape[:1] + (groups,) + by_head.shape[1:])
     pieces = pieces.reshape((groups * by_head.shape[0],) + by_head.shape[1:])
     half = lax.all_to_all(pieces, spread_axes, 0, 0, tiled=True)
     half = half.reshape((-1,) + half.shape[2:])

time: 102 us -> 103 us (level)
  the two profiles are of different devices: /device:TPU:16 before, /device:TPU:8 now
where the time goes in v8:
time: 103 us; the launch traced here: 102 us
  waiting for transfers between devices  40.1 us (39%)
  starting transfers between devices  24.7 us (24%)
  Pallas kernels  21 us (20%)
  local copies, waits for them, and re-layouts  7.35 us (7%)
  blocking collectives  5.42 us (5%)
  between operations  3.14 us (3%)
    all_to_all x1, waiting for transfers between devices, per_device(): half = lax.all_to_all(pieces, spread_axes, 0, 0, tiled=True)  30 us
    all_to_all x1, starting transfers between devices, per_device(): half = lax.all_to_all(pieces, spread_axes, 0, 0, tiled=True)  21.3 us
    pallas_call x1, Pallas kernels, attend(): pl.pallas_call(kernel, grid=(heads,), in_specs=[pl.BlockSpec(memory_space...  21 us
    all_to_all x1, waiting for transfers between devices, per_device(): summed = jnp.sum(lax.all_to_all(spread, mp_axes, 0, 0, tiled=True)[:, 0])  10.1 us
    all_to_all x1, blocking collectives, gather_by_all_to_all(): got = lax.all_to_all(copies, axes, 0, 0, tiled=True)  5.42 us
    all_to_all x1, starting transfers between devices, per_device(): summed = jnp.sum(lax.all_to_all(spread, mp_axes, 0, 0, tiled=True)[:, 0])  3.36 us
    unnamed x7, local copies, waits for them, and re-layouts  2.3 us
  transfers between devices with their start and end apart: 2, of which 2 were waited for; matrix products, arithmetic and copies ran while one was open for 2% of the time, Pallas kernels for 0%

profile of v8, /device:TPU:8, one launch (start us, length us, event | category | flops | bytes accessed | tf_op | source)
XLA Modules:
  0.0 102.3 jit_solution(12116384261882171181)
XLA Ops:
  0.6 0.0 copy-start.1
  0.6 0.0 copy-start
  0.6 0.8 copy.17
  1.5 1.1 %broadcast_in_dim.6 = bf16[8,32,8,2,128]{4,2,3,1,0:T(8,128)(2,1)} broadcast(bf16[8,8,2,128]{3,1,2,0:T(8,128)(2,1)S(1)} %copy.17), dimensions={0,2,3,4} | broadcast | bytes 1081344 | tf_op jit(solution)/shard_map/broadcast_in_dim | solution.py:98
  2.6 21.3 %all-to-all-start = ((bf16[256,8,2,128]{3,1,2,0:T(8,128)(2,1)}), bf16[256,8,2,128]{3,1,2,0:T(8,128)(2,1)S(1)}, u32[]{:S(2)}, u32[]{:S(2)}) async-start(bf16[256,8,2,128]{3,1,2,0:T(8,128)(2,1)} %bitcast.1), calls=%async_computation | async-start | bytes 2097152 | tf_op jit(solution)/shard_map/all_to_all | solution.py:100
  23.9 0.0 copy-done.1
  23.9 0.2 fusion
  24.1 0.6 copy.32
  24.8 0.7 copy.24
  26.2 0.0 copy-done
  26.2 0.9 copy.31
  27.1 30.0 %all-to-all-done = bf16[256,8,2,128]{3,1,2,0:T(8,128)(2,1)S(1)} async-done(((bf16[256,8,2,128]{3,1,2,0:T(8,128)(2,1)}), bf16[256,8,2,128]{3,1,2,0:T(8,128)(2,1)S(1)}, u32[]{:S(2)}, u32[]{:S(2)}) %all-to-all-start) | async-done | bytes 1048608 | tf_op jit(solution)/shard_map/all_to_all | solution.py:100
  57.1 0.1 copy.30
  57.2 0.3 broadcast_in_dim.15
  57.4 5.4 %all_to_all.22 = bf16[2,2048,2,128]{3,1,2,0:T(8,128)(2,1)S(1)} all-to-all(bf16[2,2048,2,128]{3,1,2,0:T(8,128)(2,1)S(1)} %broadcast_in_dim.15), channel_id=1, replica_groups=mesh['y_lo'=4,'z'=8,'core'=2,'y_hi'=2,'x'=4] {'core'}, dimensions={0} | all-to-all | bytes 4194304 | tf_op jit(solution)/shard_map/all_to_all | solution.py:24
  62.9 0.1 copy.19
  63.0 1.1 %slice_bitcast_fusion = (bf16[4096,128]{1,0:T(8,128)(2,1)}, bf16[128,4096]{0,1:T(8,128)(2,1)S(1)}) fusion(bf16[4096,2,128]{2,0,1:T(8,128)(2,1)S(1)} %bitcast.29), kind=kLoop, calls=%fused_computation | loop fusion | bytes 4194304 | tf_op jit(solution)/shard_map/squeeze | solution.py:104
  64.1 1.3 %copy.22.far_keys_ref = bf16[128,4096]{1,0:T(8,128)(2,1)} copy(bf16[128,4096]{0,1:T(8,128)(2,1)S(1)} %get-tuple-element.7) | data formatting | bytes 2097152 | tf_op jit(solution)/shard_map/transpose | solution.py:103
  65.4 21.0 %shard_map.68 = (bf16[256,1024]{1,0:T(8,128)(2,1)}, f32[8,128]{1,0:T(8,128)}) custom-call(s32[1]{0:T(128)S(6)} %copy.33.length_ref, bf16[256,1024]{1,0:T(8,128)(2,1)} %bitcast.31, bf16[128,4096]{1,0:T(8,128)(2,1)} %copy.22.far_keys_ref, bf16[4096,128]{1,0:T(8,128)(2,1)} %get-tuple-element.6.far_values_ref, bf16[128,256]{1,0:T(8,128)(2,1)} %bitcast.34, ...), custom_call_target="tpu_custom_call" | custom-call | tf_op jit(solution)/shard_map/pallas_call | solution.py:69
  86.5 3.4 %all-to-all-start.2 = ((f32[8,1,128]{2,1,0:T(1,128)}), f32[8,1,128]{2,1,0:T(1,128)S(1)}, u32[]{:S(2)}, u32[]{:S(2)}) async-start(f32[8,1,128]{2,1,0:T(1,128)} %bitcast.38), calls=%async_computation.2 | async-start | bytes 8192 | tf_op jit(solution)/shard_map/all_to_all | solution.py:109
  89.8 10.1 %all-to-all-done.2 = f32[8,1,128]{2,1,0:T(1,128)S(1)} async-done(((f32[8,1,128]{2,1,0:T(1,128)}), f32[8,1,128]{2,1,0:T(1,128)S(1)}, u32[]{:S(2)}, u32[]{:S(2)}) %all-to-all-start.2) | async-done | bytes 4128 | tf_op jit(solution)/shard_map/all_to_all | solution.py:109
  99.9 0.6 slice_reduce_fusion
Async XLA Ops:
  0.6 23.3 %copy-start.1 = (bf16[256,2,1,128]{3,1,2,0:T(2,128)(2,1)S(1)}, bf16[256,2,1,128]{3,1,2,0:T(2,128)(2,1)}, u32[]{:S(2)}) copy-start(bf16[256,2,1,128]{3,1,2,0:T(2,128)(2,1)} %param.6) | copy-start | bytes 393220
  0.6 25.5 %copy-start = (bf16[256,8,128]{2,1,0:T(8,128)(2,1)S(1)}, bf16[256,8,128]{2,1,0:T(8,128)(2,1)}, u32[]{:S(2)}) copy-start(bf16[256,8,128]{2,1,0:T(8,128)(2,1)} %param.5) | copy-start | bytes 1572868
  2.6 54.5 %all-to-all-start = ((bf16[256,8,2,128]{3,1,2,0:T(8,128)(2,1)}), bf16[256,8,2,128]{3,1,2,0:T(8,128)(2,1)S(1)}, u32[]{:S(2)}, u32[]{:S(2)}) async-start(bf16[256,8,2,128]{3,1,2,0:T(8,128)(2,1)} %bitcast.1), calls=%async_computation | async-start | bytes 2097152 | tf_op jit(solution)/shard_map/all_to_all | solution.py:100
  86.5 13.5 %all-to-all-start.2 = ((f32[8,1,128]{2,1,0:T(1,128)}), f32[8,1,128]{2,1,0:T(1,128)S(1)}, u32[]{:S(2)}, u32[]{:S(2)}) async-start(f32[8,1,128]{2,1,0:T(1,128)} %bitcast.38), calls=%async_computation.2 | async-start | bytes 8192 | tf_op jit(solution)/shard_map/all_to_all | solution.py:109

commit v9 on v6

--- a/solution.py
+++ b/solution.py
@@ -26,21 +26,18 @@
     return got.reshape((count * x.shape[0],) + x.shape[1:])
 
 
-def first_kernel(length_ref, q_ref, far_keys_ref, far_values_ref, near_keys_ref, near_values_ref, top_ref, total_ref, accum_ref, *, factor):
+def first_kernel(length_ref, q_ref, near_keys_ref, near_values_ref, top_ref, total_ref, accum_ref, *, factor):
     length = length_ref[0]
     q = q_ref[...]
-    far = jnp.dot(q, far_keys_ref[...], preferred_element_type=jnp.float32) * factor
     near = jnp.dot(q, near_keys_ref[...], preferred_element_type=jnp.float32) * factor
     query_pos = lax.broadcasted_iota(jnp.int32, near.shape, 0)
     key_pos = lax.broadcasted_iota(jnp.int32, near.shape, 1)
     allowed = (key_pos <= query_pos) & (key_pos < length)
     near = jnp.where(allowed, near, neg_large)
-    top = jnp.maximum(jnp.max(far, axis=1, keepdims=True), jnp.max(near, axis=1, keepdims=True))
-    far_w = jnp.exp(far - top)
+    top = jnp.max(near, axis=1, keepdims=True)
     near_w = jnp.where(allowed, jnp.exp(near - top), 0.0)
-    total = jnp.sum(far_w, axis=1, keepdims=True) + jnp.sum(near_w, axis=1, keepdims=True)
-    mixed = jnp.dot(far_w.astype(jnp.bfloat16), far_values_ref[...], preferred_element_type=jnp.float32)
-    mixed = mixed + jnp.dot(near_w.astype(jnp.bfloat16), near_values_ref[...], preferred_element_type=jnp.float32)
+    total = jnp.sum(near_w, axis=1, keepdims=True)
+    mixed = jnp.dot(near_w.astype(jnp.bfloat16), near_values_ref[...], preferred_element_type=jnp.float32)
     top_ref[...] = jnp.broadcast_to(top, top_ref.shape)
     total_ref[...] = jnp.broadcast_to(total, total_ref.shape)
     accum_ref[...] = mixed
@@ -76,10 +73,9 @@
         part_ref[...] = jnp.broadcast_to(jnp.sum(part_ref[...]), part_ref.shape)
 
 
-def attend_first(lengths, flat, far_keys_t, far_values, near_keys_t, near_values, head_size):
+def attend_first(lengths, flat, near_keys_t, near_values, head_size):
     tokens = flat.shape[0]
     heads = flat.shape[1] // head_size
-    keys = far_values.shape[0]
     kernel = functools.partial(first_kernel, factor=1.0 / math.sqrt(head_size))
     whole = lambda h: (0, 0)
     per_head = pl.BlockSpec((tokens, head_size), lambda h: (0, h))
@@ -90,14 +86,12 @@
         in_specs=[
             pl.BlockSpec(memory_space=pltpu.SMEM),
             per_head,
-            pl.BlockSpec((head_size, keys), whole),
-            pl.BlockSpec((keys, head_size), whole),
             pl.BlockSpec((head_size, tokens), whole),
             pl.BlockSpec((tokens, head_size), whole),
         ],
         out_specs=[per_head, per_head, per_head],
         out_shape=[state, state, state],
-    )(lengths, flat, far_keys_t, far_values, near_keys_t, near_values)
+    )(lengths, flat, near_keys_t, near_values)
 
 
 def attend_second(lengths, flat, far_keys_t, far_values, top, total, accum, score_weight, head_size, copies):
@@ -143,15 +137,13 @@
     resp_len, local_heads, head_size = queries.shape
     length = lengths[0]
     by_head = jnp.transpose(prefix_kv, (2, 0, 1, 3))
-    split = by_head.shape[1] // 2
-    keys_a, values_a = fetch_prompt(by_head[:, :split])
-    keys_b, values_b = fetch_prompt(by_head[:, split:])
+    keys, values = fetch_prompt(by_head)
     flat = queries.reshape(resp_len, local_heads * head_size)
     near_keys_t = response_kv[:, 0, 0].T
     near_values = response_kv[:, 1, 0]
-    top, total, accum = attend_first(lengths, flat, keys_a, values_a, near_keys_t, near_values, head_size)
+    top, total, accum = attend_first(lengths, flat, near_keys_t, near_values, head_size)
     copies = axis_size["y_hi"] * axis_size["x"]
-    attended, spread = attend_second(lengths, flat, keys_b, values_b, top, total, accum, score_weight, head_size, copies)
+    attended, spread = attend_second(lengths, flat, keys, values, top, total, accum, score_weight, head_size, copies)
     summed = jnp.sum(lax.all_to_all(spread, mp_axes, 0, 0, tiled=True)[:, 0])
     score = (summed / length.astype(jnp.float32)).reshape(1)
     return (attended, score)

time: 130 us -> 102 us (0.78)
  waiting for transfers between devices: 45.2 us -> 30.7 us
  starting transfers between devices: 35.7 us -> 27 us
  blocking collectives: 9.15 us -> 5.42 us
  local copies, waits for them, and re-layouts: 9.86 us -> 7.44 us
    all_to_all x2 -> x1, waiting for transfers between devices: 35.1 us -> 20.6 us  [fetch_prompt(): half = lax.all_to_all(pieces, spread_axes, 0, 0, tiled=True)]
    all_to_all x2 -> x1, starting transfers between devices: 31.3 us -> 22 us  [fetch_prompt(): half = lax.all_to_all(pieces, spread_axes, 0, 0, tiled=True)]
    pallas_call x1, Pallas kernels: 12.8 us -> 19.9 us  [attend_second(): pl.pallas_call(kernel, grid=(heads,), in_specs=[pl.BlockSpec(memory_space...]
    pallas_call x1, Pallas kernels: 12.6 us -> 6.6 us  [attend_first(): pl.pallas_call(kernel, grid=(heads,), in_specs=[pl.BlockSpec(memory_space...]
    all_to_all x2 -> x1, blocking collectives: 9.15 us -> 5.42 us  [gather_by_all_to_all(): got = lax.all_to_all(copies, axes, 0, 0, tiled=True)]
  transfers between devices with their start and end apart: 3 -> 2, of which waited for: 3 -> 2; matrix products, arithmetic and copies ran while one was open for 3% -> 2% of each run, Pallas kernels for 0% -> 7%
where the time goes in v9:
time: 102 us; the launch traced here: 101 us
  waiting for transfers between devices  30.7 us (30%)
  starting transfers between devices  27 us (26%)
  Pallas kernels  26.5 us (26%)
  local copies, waits for them, and re-layouts  7.44 us (7%)
  blocking collectives  5.42 us (5%)
  between operations  3.12 us (3%)
    all_to_all x1, starting transfers between devices, fetch_prompt(): half = lax.all_to_all(pieces, spread_axes, 0, 0, tiled=True)  22 us
    all_to_all x1, waiting for transfers between devices, fetch_prompt(): half = lax.all_to_all(pieces, spread_axes, 0, 0, tiled=True)  20.6 us
    pallas_call x1, Pallas kernels, attend_second(): pl.pallas_call(kernel, grid=(heads,), in_specs=[pl.BlockSpec(memory_space...  19.9 us
    all_to_all x1, waiting for transfers between devices, per_device_body(): summed = jnp.sum(lax.all_to_all(spread, mp_axes, 0, 0, tiled=True)[:, 0])  10.1 us
    pallas_call x1, Pallas kernels, attend_first(): pl.pallas_call(kernel, grid=(heads,), in_specs=[pl.BlockSpec(memory_space...  6.6 us
    all_to_all x1, blocking collectives, gather_by_all_to_all(): got = lax.all_to_all(copies, axes, 0, 0, tiled=True)  5.42 us
    all_to_all x1, starting transfers between devices, per_device_body(): summed = jnp.sum(lax.all_to_all(spread, mp_axes, 0, 0, tiled=True)[:, 0])  5.01 us
    unnamed x7, local copies, waits for them, and re-layouts  2.3 us
  transfers between devices with their start and end apart: 2, of which 2 were waited for; matrix products, arithmetic and copies ran while one was open for 2% of the time, Pallas kernels for 7%

profile of v9, /device:TPU:16, one launch (start us, length us, event | category | flops | bytes accessed | tf_op | source)
XLA Modules:
  0.0 100.8 jit_solution(818750764373257973)
XLA Ops:
  0.6 0.0 copy-start
  0.6 0.8 copy.17
  1.5 0.0 copy-start.1
  1.5 1.2 %broadcast_in_dim.6 = bf16[32,8,8,2,128]{4,2,3,1,0:T(8,128)(2,1)} broadcast(bf16[8,8,2,128]{3,1,2,0:T(8,128)(2,1)S(1)} %copy.17), dimensions={1,2,3,4} | broadcast | bytes 1081344 | tf_op jit(solution)/shard_map/broadcast_in_dim | solution.py:128
  2.7 22.0 %all-to-all-start = ((bf16[256,8,2,128]{3,1,2,0:T(8,128)(2,1)}), bf16[256,8,2,128]{3,1,2,0:T(8,128)(2,1)S(1)}, u32[]{:S(2)}, u32[]{:S(2)}) async-start(bf16[256,8,2,128]{3,1,2,0:T(8,128)(2,1)} %bitcast.1), calls=%async_computation | async-start | bytes 2097152 | tf_op jit(solution)/shard_map/all_to_all | solution.py:130
  25.3 0.0 copy-done
  25.3 0.9 copy.31
  26.3 0.0 copy-done.1
  26.3 0.2 fusion
  26.4 0.7 copy.24
  27.2 0.6 copy.32
  27.8 6.6 %shard_map.68 = (f32[256,1024]{1,0:T(8,128)}, f32[256,1024]{1,0:T(8,128)}, f32[256,1024]{1,0:T(8,128)}) custom-call(s32[1]{0:T(128)S(6)} %copy.33.length_ref, bf16[256,1024]{1,0:T(8,128)(2,1)} %bitcast.30, bf16[128,256]{1,0:T(8,128)(2,1)} %bitcast.34, bf16[256,128]{1,0:T(8,128)(2,1)} %bitcast.35), custom_call_target="tpu_custom_call" | custom-call | tf_op jit(solution)/shard_map/pallas_call | solution.py:83
  34.4 20.6 %all-to-all-done = bf16[256,8,2,128]{3,1,2,0:T(8,128)(2,1)S(1)} async-done(((bf16[256,8,2,128]{3,1,2,0:T(8,128)(2,1)}), bf16[256,8,2,128]{3,1,2,0:T(8,128)(2,1)S(1)}, u32[]{:S(2)}, u32[]{:S(2)}) %all-to-all-start) | async-done | bytes 1048608 | tf_op jit(solution)/shard_map/all_to_all | solution.py:130
  55.1 0.1 copy.30
  55.1 0.3 broadcast_in_dim.15
  55.4 5.4 %all_to_all.22 = bf16[2,2048,2,128]{3,1,2,0:T(8,128)(2,1)S(1)} all-to-all(bf16[2,2048,2,128]{3,1,2,0:T(8,128)(2,1)S(1)} %broadcast_in_dim.15), channel_id=1, replica_groups=mesh['y_lo'=4,'z'=8,'core'=2,'y_hi'=2,'x'=4] {'core'}, dimensions={0} | all-to-all | bytes 4194304 | tf_op jit(solution)/shard_map/all_to_all | solution.py:25
  60.8 0.1 copy.19
  61.0 1.1 %slice_bitcast_fusion = (bf16[4096,128]{1,0:T(8,128)(2,1)}, bf16[128,4096]{0,1:T(8,128)(2,1)S(1)}) fusion(bf16[4096,2,128]{2,0,1:T(8,128)(2,1)S(1)} %bitcast.29), kind=kLoop, calls=%fused_computation | loop fusion | bytes 4194304 | tf_op jit(solution)/shard_map/squeeze | solution.py:133
  62.1 1.3 %copy.22.far_keys_ref = bf16[128,4096]{1,0:T(8,128)(2,1)} copy(bf16[128,4096]{0,1:T(8,128)(2,1)S(1)} %get-tuple-element.13) | data formatting | bytes 2097152 | tf_op jit(solution)/shard_map/transpose | solution.py:133
  63.4 19.9 %shard_map.69 = (bf16[256,1024]{1,0:T(8,128)(2,1)}, f32[8,128]{1,0:T(8,128)}) custom-call(s32[1]{0:T(128)S(6)} %copy.33.length_ref, bf16[256,1024]{1,0:T(8,128)(2,1)} %bitcast.31, bf16[128,4096]{1,0:T(8,128)(2,1)} %copy.22.far_keys_ref, bf16[4096,128]{1,0:T(8,128)(2,1)} %get-tuple-element.12.far_values_ref, f32[256,1024]{1,0:T(8,128)} %get-tuple-element.7.top_ref, ...), custom_call_target="tpu_custom_call" | custom-call | tf_op jit(solution)/shard_map/pallas_call | solution.py:104
  83.3 5.0 %all-to-all-start.2 = ((f32[8,1,128]{2,1,0:T(1,128)}), f32[8,1,128]{2,1,0:T(1,128)S(1)}, u32[]{:S(2)}, u32[]{:S(2)}) async-start(f32[8,1,128]{2,1,0:T(1,128)} %bitcast.38), calls=%async_computation.2 | async-start | bytes 8192 | tf_op jit(solution)/shard_map/all_to_all | solution.py:147
  88.4 10.1 %all-to-all-done.2 = f32[8,1,128]{2,1,0:T(1,128)S(1)} async-done(((f32[8,1,128]{2,1,0:T(1,128)}), f32[8,1,128]{2,1,0:T(1,128)S(1)}, u32[]{:S(2)}, u32[]{:S(2)}) %all-to-all-start.2) | async-done | bytes 4128 | tf_op jit(solution)/shard_map/all_to_all | solution.py:147
  98.4 0.6 slice_reduce_fusion
Async XLA Ops:
  0.6 24.7 %copy-start = (bf16[256,8,128]{2,1,0:T(8,128)(2,1)S(1)}, bf16[256,8,128]{2,1,0:T(8,128)(2,1)}, u32[]{:S(2)}) copy-start(bf16[256,8,128]{2,1,0:T(8,128)(2,1)} %param.5) | copy-start | bytes 1572868
  1.5 24.8 %copy-start.1 = (bf16[256,2,1,128]{3,1,2,0:T(2,128)(2,1)S(1)}, bf16[256,2,1,128]{3,1,2,0:T(2,128)(2,1)}, u32[]{:S(2)}) copy-start(bf16[256,2,1,128]{3,1,2,0:T(2,128)(2,1)} %param.6) | copy-start | bytes 393220
  2.7 52.4 %all-to-all-start = ((bf16[256,8,2,128]{3,1,2,0:T(8,128)(2,1)}), bf16[256,8,2,128]{3,1,2,0:T(8,128)(2,1)S(1)}, u32[]{:S(2)}, u32[]{:S(2)}) async-start(bf16[256,8,2,128]{3,1,2,0:T(8,128)(2,1)} %bitcast.1), calls=%async_computation | async-start | bytes 2097152 | tf_op jit(solution)/shard_map/all_to_all | solution.py:130
  83.3 15.1 %all-to-all-start.2 = ((f32[8,1,128]{2,1,0:T(1,128)}), f32[8,1,128]{2,1,0:T(1,128)S(1)}, u32[]{:S(2)}, u32[]{:S(2)}) async-start(f32[8,1,128]{2,1,0:T(1,128)} %bitcast.38), calls=%async_computation.2 | async-start | bytes 8192 | tf_op jit(solution)/shard_map/all_to_all | solution.py:147

commit v10 on v9

--- a/solution.py
+++ b/solution.py
@@ -47,7 +47,8 @@
     head = pl.program_id(0)
     length = length_ref[0]
     q = q_ref[...]
-    far = jnp.dot(q, far_keys_ref[...], preferred_element_type=jnp.float32) * factor
+    contract = (((1,), (1,)), ((), ()))
+    far = lax.dot_general(q, far_keys_ref[...], contract, preferred_element_type=jnp.float32) * factor
     before = top_ref[:, :1]
     top = jnp.maximum(before, jnp.max(far, axis=1, keepdims=True))
     shrink = jnp.exp(before - top)
@@ -94,7 +95,7 @@
     )(lengths, flat, near_keys_t, near_values)
 
 
-def attend_second(lengths, flat, far_keys_t, far_values, top, total, accum, score_weight, head_size, copies):
+def attend_second(lengths, flat, far_keys, far_values, top, total, accum, score_weight, head_size, copies):
     tokens = flat.shape[0]
     heads = flat.shape[1] // head_size
     keys = far_values.shape[0]
@@ -107,7 +108,7 @@
         in_specs=[
             pl.BlockSpec(memory_space=pltpu.SMEM),
             per_head,
-            pl.BlockSpec((head_size, keys), whole),
+            pl.BlockSpec((keys, head_size), whole),
             pl.BlockSpec((keys, head_size), whole),
             per_head,
             per_head,
@@ -119,7 +120,7 @@
             jax.ShapeDtypeStruct((tokens, heads * head_size), jnp.bfloat16),
             jax.ShapeDtypeStruct((copies, head_size), jnp.float32),
         ],
-    )(lengths, flat, far_keys_t, far_values, top, total, accum, score_weight.reshape(1, -1))
+    )(lengths, flat, far_keys, far_values, top, total, accum, score_weight.reshape(1, -1))
 
 
 def fetch_prompt(by_head):
@@ -128,15 +129,16 @@
     pieces = jnp.broadcast_to(by_head[None], (groups,) + by_head.shape)
     pieces = pieces.reshape((groups * by_head.shape[0],) + by_head.shape[1:])
     half = lax.all_to_all(pieces, spread_axes, 0, 0, tiled=True)
-    half = half.reshape((-1,) + half.shape[2:])
-    collected = gather_by_all_to_all(half, ("core",))
-    return collected[:, 0].T, collected[:, 1]
+    both = gather_by_all_to_all(half[None], ("core",))
+    keys = both[:, :, 0].reshape(-1, both.shape[-1])
+    values = both[:, :, 1].reshape(-1, both.shape[-1])
+    return keys, values
 
 
 def per_device_body(queries, response_kv, prefix_kv, lengths, score_weight):
     resp_len, local_heads, head_size = queries.shape
     length = lengths[0]
-    by_head = jnp.transpose(prefix_kv, (2, 0, 1, 3))
+    by_head = jnp.transpose(prefix_kv, (2, 1, 0, 3))
     keys, values = fetch_prompt(by_head)
     flat = queries.reshape(resp_len, local_heads * head_size)
     near_keys_t = response_kv[:, 0, 0].T

time: 102 us -> 101 us (level)
  local copies, waits for them, and re-layouts: 7.44 us -> 6.36 us
    slice x0 -> x1, local copies, waits for them, and re-layouts: none -> 1.49 us  [fetch_prompt(): values = both[:, :, 1].reshape(-1, both.shape[-1])]
    transpose x2 -> x1, local copies, waits for them, and re-layouts: 2.14 us -> 0.83 us  [per_device_body(): by_head = jnp.transpose(prefix_kv, (2, 1, 0, 3))]
    squeeze x1 -> x0, local copies, waits for them, and re-layouts: 1.12 us -> none  [fetch_prompt(): return (collected[:, 0].T, collected[:, 1])]
where the time goes in v10:
time: 101 us; the launch traced here: 100 us
  waiting for transfers between devices  30.7 us (30%)
  starting transfers between devices  27 us (27%)
  Pallas kernels  27 us (27%)
  local copies, waits for them, and re-layouts  6.36 us (6%)
  blocking collectives  5.42 us (5%)
  between operations  3.12 us (3%)
    all_to_all x1, starting transfers between devices, fetch_prompt(): half = lax.all_to_all(pieces, spread_axes, 0, 0, tiled=True)  22 us
    all_to_all x1, waiting for transfers between devices, fetch_prompt(): half = lax.all_to_all(pieces, spread_axes, 0, 0, tiled=True)  20.6 us
    pallas_call x1, Pallas kernels, attend_second(): pl.pallas_call(kernel, grid=(heads,), in_specs=[pl.BlockSpec(memory_space...  20.4 us
    all_to_all x1, waiting for transfers between devices, per_device_body(): summed = jnp.sum(lax.all_to_all(spread, mp_axes, 0, 0, tiled=True)[:, 0])  10.1 us
    pallas_call x1, Pallas kernels, attend_first(): pl.pallas_call(kernel, grid=(heads,), in_specs=[pl.BlockSpec(memory_space...  6.6 us
    all_to_all x1, blocking collectives, gather_by_all_to_all(): got = lax.all_to_all(copies, axes, 0, 0, tiled=True)  5.42 us
    all_to_all x1, starting transfers between devices, per_device_body(): summed = jnp.sum(lax.all_to_all(spread, mp_axes, 0, 0, tiled=True)[:, 0])  5.01 us
    unnamed x7, local copies, waits for them, and re-layouts  2.3 us
  transfers between devices with their start and end apart: 2, of which 2 were waited for; matrix products, arithmetic and copies ran while one was open for 2% of the time, Pallas kernels for 7%

profile of v10, /device:TPU:16, one launch (start us, length us, event | category | flops | bytes accessed | tf_op | source)
XLA Modules:
  0.0 100.2 jit_solution(8520112343518112950)
XLA Ops:
  0.6 0.0 copy-start
  0.6 0.8 copy.10
  1.5 0.0 copy-start.1
  1.5 1.2 %broadcast_in_dim.4 = bf16[32,8,2,8,128]{4,3,2,1,0:T(8,128)(2,1)} broadcast(bf16[8,2,8,128]{3,2,1,0:T(8,128)(2,1)S(1)} %copy.10), dimensions={1,2,3,4} | broadcast | bytes 1081344 | tf_op jit(solution)/shard_map/broadcast_in_dim | solution.py:129
  2.7 22.0 %all-to-all-start = ((bf16[256,2,8,128]{3,2,1,0:T(8,128)(2,1)}), bf16[256,2,8,128]{3,2,1,0:T(8,128)(2,1)S(1)}, u32[]{:S(2)}, u32[]{:S(2)}) async-start(bf16[256,2,8,128]{3,2,1,0:T(8,128)(2,1)} %bitcast.1), calls=%async_computation | async-start | bytes 2097152 | tf_op jit(solution)/shard_map/all_to_all | solution.py:131
  25.3 0.0 copy-done
  25.3 0.9 copy.20
  26.3 0.0 copy-done.1
  26.3 0.2 fusion.1
  26.4 0.7 copy.15
  27.2 0.6 copy.21
  27.8 6.6 %shard_map.68 = (f32[256,1024]{1,0:T(8,128)}, f32[256,1024]{1,0:T(8,128)}, f32[256,1024]{1,0:T(8,128)}) custom-call(s32[1]{0:T(128)S(6)} %copy.22.length_ref, bf16[256,1024]{1,0:T(8,128)(2,1)} %bitcast.23, bf16[128,256]{1,0:T(8,128)(2,1)} %bitcast.28, bf16[256,128]{1,0:T(8,128)(2,1)} %bitcast.29), custom_call_target="tpu_custom_call" | custom-call | tf_op jit(solution)/shard_map/pallas_call | solution.py:84
  34.4 20.6 %all-to-all-done = bf16[256,2,8,128]{3,2,1,0:T(8,128)(2,1)S(1)} async-done(((bf16[256,2,8,128]{3,2,1,0:T(8,128)(2,1)}), bf16[256,2,8,128]{3,2,1,0:T(8,128)(2,1)S(1)}, u32[]{:S(2)}, u32[]{:S(2)}) %all-to-all-start) | async-done | bytes 1048608 | tf_op jit(solution)/shard_map/all_to_all | solution.py:131
  55.1 0.1 copy.11
  55.1 0.3 broadcast_in_dim.5
  55.4 5.4 %all_to_all.22 = bf16[2,1,256,2,8,128]{5,4,2,3,1,0:T(8,128)(2,1)S(1)} all-to-all(bf16[2,1,256,2,8,128]{5,4,2,3,1,0:T(8,128)(2,1)S(1)} %broadcast_in_dim.5), channel_id=1, replica_groups=mesh['y_lo'=4,'z'=8,'core'=2,'y_hi'=2,'x'=4] {'core'}, dimensions={0} | all-to-all | bytes 4194304 | tf_op jit(solution)/shard_map/all_to_all | solution.py:25
  60.8 1.5 %fusion = (bf16[2,256,1,8,128]{4,3,1,2,0:T(8,128)(2,1)}, bf16[2,256,1,8,128]{4,3,1,2,0:T(8,128)(2,1)}) fusion(bf16[2,256,2,8,128]{4,3,1,2,0:T(8,128)(2,1)S(1)} %bitcast.22), kind=kLoop, calls=%fused_computation.3 | loop fusion | bytes 4194304 | tf_op jit(solution)/shard_map/slice | solution.py:134
  62.3 20.4 %shard_map.69 = (bf16[256,1024]{1,0:T(8,128)(2,1)}, f32[8,128]{1,0:T(8,128)}) custom-call(s32[1]{0:T(128)S(6)} %copy.22.length_ref, bf16[256,1024]{1,0:T(8,128)(2,1)} %bitcast.24, bf16[4096,128]{1,0:T(8,128)(2,1)} %bitcast.26, bf16[4096,128]{1,0:T(8,128)(2,1)} %bitcast.25, f32[256,1024]{1,0:T(8,128)} %get-tuple-element.7.top_ref, ...), custom_call_target="tpu_custom_call" | custom-call | tf_op jit(solution)/shard_map/pallas_call | solution.py:105
  82.7 5.0 %all-to-all-start.2 = ((f32[8,1,128]{2,1,0:T(1,128)}), f32[8,1,128]{2,1,0:T(1,128)S(1)}, u32[]{:S(2)}, u32[]{:S(2)}) async-start(f32[8,1,128]{2,1,0:T(1,128)} %bitcast.32), calls=%async_computation.2 | async-start | bytes 8192 | tf_op jit(solution)/shard_map/all_to_all | solution.py:149
  87.7 10.1 %all-to-all-done.2 = f32[8,1,128]{2,1,0:T(1,128)S(1)} async-done(((f32[8,1,128]{2,1,0:T(1,128)}), f32[8,1,128]{2,1,0:T(1,128)S(1)}, u32[]{:S(2)}, u32[]{:S(2)}) %all-to-all-start.2) | async-done | bytes 4128 | tf_op jit(solution)/shard_map/all_to_all | solution.py:149
  97.8 0.6 slice_reduce_fusion
Async XLA Ops:
  0.6 24.7 %copy-start = (bf16[256,8,128]{2,1,0:T(8,128)(2,1)S(1)}, bf16[256,8,128]{2,1,0:T(8,128)(2,1)}, u32[]{:S(2)}) copy-start(bf16[256,8,128]{2,1,0:T(8,128)(2,1)} %param.5) | copy-start | bytes 1572868
  1.5 24.8 %copy-start.1 = (bf16[256,2,1,128]{3,1,2,0:T(2,128)(2,1)S(1)}, bf16[256,2,1,128]{3,1,2,0:T(2,128)(2,1)}, u32[]{:S(2)}) copy-start(bf16[256,2,1,128]{3,1,2,0:T(2,128)(2,1)} %param.6) | copy-start | bytes 393220
  2.7 52.4 %all-to-all-start = ((bf16[256,2,8,128]{3,2,1,0:T(8,128)(2,1)}), bf16[256,2,8,128]{3,2,1,0:T(8,128)(2,1)S(1)}, u32[]{:S(2)}, u32[]{:S(2)}) async-start(bf16[256,2,8,128]{3,2,1,0:T(8,128)(2,1)} %bitcast.1), calls=%async_computation | async-start | bytes 2097152 | tf_op jit(solution)/shard_map/all_to_all | solution.py:131
  82.7 15.1 %all-to-all-start.2 = ((f32[8,1,128]{2,1,0:T(1,128)}), f32[8,1,128]{2,1,0:T(1,128)S(1)}, u32[]{:S(2)}, u32[]{:S(2)}) async-start(f32[8,1,128]{2,1,0:T(1,128)} %bitcast.32), calls=%async_computation.2 | async-start | bytes 8192 | tf_op jit(solution)/shard_map/all_to_all | solution.py:149
